TPU v7x, 128 devices: a whole 4x4x4 slice. The times are simulated.
128 devices in a mesh: chan: 32 (over z, y_lo, x), freq: 4 (over y_hi, core).
Axes of the slice: x: 4, y: 4 (y_hi: 2, y_lo: 2; y = y_hi * 2 + y_lo), z: 4, core: 2. Of those that a mesh axis runs over, the one named last changes fastest.
Arguments:
- strain: bfloat16 [2048, 256, 1024], P('chan', 'freq'), may hold values from -6 to 6
- mad_index: int32 [2048], P('chan'), may hold values from 0 to 15
- mad_table: float32 [16], replicated, may hold values from 0.25 to 2.5
- freq_bins: int32 [64], replicated, may hold values from 1 to 511
- valid_count: int32 [2048], P('chan'), may hold values from 64 to 256
Outputs:
- cross: float32 [64, 2, 2048, 2048], P('freq', None, 'chan')
All inputs are finite; a program needn't handle non-finite values.
Results may differ from a plain program's by a relative error of at most 0.0057.
Values may be sent and summed in bfloat16 or wider, within the bound.
No kernel may reach another device: no remote copies, remote signals or barrier semaphores. Data moves between devices by JAX's collectives and lax.ppermute only.
A program may use at most 256 MiB of HBM per device.

v0:
```python
import math

import jax
import jax.numpy as jnp
from jax import lax
from jax.sharding import Mesh, PartitionSpec as P

CLIP_FACTOR = 2.0


def dft_table(freq_bins, length):
    samples = jnp.arange(length, dtype=jnp.int32)
    phase_index = samples[:, None] * freq_bins[None, :] % length
    angle = phase_index.astype(jnp.float32) * (2.0 * math.pi / length)
    taper = 0.5 - 0.5 * jnp.cos(samples.astype(jnp.float32) * (2.0 * math.pi / length))
    cosine = taper[:, None] * jnp.cos(angle)
    sine = -taper[:, None] * jnp.sin(angle)
    stacked = jnp.stack([cosine, sine], axis=2)
    return stacked.reshape(length, 2 * freq_bins.shape[0]).astype(jnp.bfloat16)


def clip_scales(mad_index, mad_table):
    entries = jnp.arange(mad_table.shape[0], dtype=jnp.int32)
    matches = mad_index[:, None] == entries[None, :]
    return jnp.sum(jnp.where(matches, mad_table[None, :], 0.0), axis=1)


def row_operand(panel):
    first, second = panel[:, 0], panel[:, 1]
    real_rows = jnp.stack([first, second], axis=2)
    imag_rows = jnp.stack([second, -first], axis=2)
    return jnp.stack([real_rows, imag_rows], axis=1)


def shifted(block, axis, distance):
    size = lax.axis_size(axis)
    return lax.ppermute(block, axis, [((i + distance) % size, i) for i in range(size)])


def ring_gather(block, axis, split_axis):
    ahead = shifted(block, axis, 1)
    behind = shifted(block, axis, -1)
    half = block.shape[split_axis] // 2
    far_a = shifted(lax.slice_in_dim(ahead, 0, half, axis=split_axis), axis, 1)
    far_b = shifted(lax.slice_in_dim(behind, half, 2 * half, axis=split_axis), axis, -1)
    far = jnp.concatenate([far_a, far_b], axis=split_axis)
    return [block, ahead, far, behind]


def ordered_by_position(slots, axis, stack_axis):
    size = len(slots)

    def arrangement(at):
        return lambda *blocks: jnp.stack(
            [blocks[(k - at) % size] for k in range(size)], axis=stack_axis
        )

    return lax.switch(lax.axis_index(axis), [arrangement(at) for at in range(size)], *slots)


def per_device(strain, mad_index, mad_table, freq_bins, valid_count):
    channels, win_local, length = strain.shape
    bin_count = freq_bins.shape[0]
    limits = (clip_scales(mad_index, mad_table) * CLIP_FACTOR)[:, None, None]
    bound = limits.astype(strain.dtype)
    clipped = jnp.minimum(jnp.maximum(strain, -bound), bound)
    table = dft_table(freq_bins, length)
    flat_rows = clipped.reshape(channels * win_local, length)
    spectrum = lax.dot_general(
        table, flat_rows, (((0,), (1,)), ((), ())), preferred_element_type=jnp.float32
    )
    freq_index = lax.axis_index("yhi") * lax.axis_size("core") + lax.axis_index("core")
    window_ids = freq_index * win_local + jnp.arange(win_local, dtype=jnp.int32)
    counts = valid_count.astype(jnp.float32)
    weights = jnp.where(
        window_ids[None, :] < valid_count[:, None], 1.0 / jnp.sqrt(counts)[:, None], 0.0
    )
    weighted = (spectrum * weights.reshape(1, channels * win_local)).astype(jnp.bfloat16)
    groups = lax.axis_size("yhi") * lax.axis_size("core")
    pairs = lax.axis_size("ylo")
    bins_local = bin_count // groups
    weighted = weighted.reshape(groups, bins_local * 2, channels * win_local)
    outgoing = jnp.broadcast_to(weighted[None], (pairs,) + weighted.shape)
    outgoing = outgoing.reshape((pairs * groups,) + weighted.shape[1:])
    incoming = lax.all_to_all(outgoing, ("ylo", "yhi", "core"), 0, 0, tiled=True)
    incoming = incoming.reshape(pairs, groups, bins_local, 2, channels, win_local)
    panel = jnp.transpose(incoming, (2, 3, 0, 4, 1, 5)).reshape(
        bins_local, 2, pairs * channels, groups * win_local
    )

    split = (bins_local * 9) // 16
    zs, xs = lax.axis_size("z"), lax.axis_size("x")
    low, high = panel[:split], panel[split:]
    first = ordered_by_position(ring_gather(low, "x", 1), "x", 0)
    second = ordered_by_position(ring_gather(high, "z", 1), "z", 0)
    at = lax.axis_index("ylo") * channels
    rows_low = row_operand(lax.dynamic_slice_in_dim(low, at, channels, axis=2))
    rows_high = row_operand(lax.dynamic_slice_in_dim(high, at, channels, axis=2))
    first, second, rows_low, rows_high = lax.optimization_barrier(
        (first, second, rows_low, rows_high)
    )
    shape = (xs, -1, 2, pairs, channels, groups * win_local)
    width = pairs * channels * xs

    def products(part, block, order):
        block = jnp.transpose(block.reshape(shape), order).reshape(-1, 2, width, groups * win_local)
        return jnp.einsum("fqipw,fpjw->fqij", part, block, preferred_element_type=jnp.float32)

    by_z = [products(rows_low, p, (1, 2, 3, 0, 4, 5)) for p in ring_gather(first, "z", 0)]
    second = [jnp.transpose(p.reshape(shape), (1, 2, 0, 3, 4, 5)) for p in ring_gather(second, "x", 0)]
    second = ordered_by_position(second, "x", 4).reshape(-1, 2, width * zs, groups * win_local)
    high = jnp.einsum(
        "fqipw,fpjw->fqij", rows_high, second, preferred_element_type=jnp.float32
    )

    def arrangement(at):
        def build(high, *blocks):
            low = jnp.concatenate([blocks[(k - at) % zs] for k in range(zs)], axis=3)
            return jnp.concatenate([low, high], axis=0)

        return build

    branches = [arrangement(at) for at in range(zs)]
    return lax.switch(lax.axis_index("z"), branches, high, *by_z)


def solution(mesh):
    sizes = dict(zip(mesh.axis_names, mesh.devices.shape))
    chan, freq = sizes["chan"], sizes["freq"]
    devices = mesh.devices.reshape(chan // 8, 2, 4, freq // 2, 2)
    grid = Mesh(devices, ("z", "ylo", "x", "yhi", "core"))
    chan_axes = ("z", "ylo", "x")
    freq_axes = ("yhi", "core")
    return jax.shard_map(
        per_device,
        mesh=grid,
        in_specs=(P(chan_axes, freq_axes, None), P(chan_axes), P(), P(), P(chan_axes)),
        out_specs=P(freq_axes, None, chan_axes, None),
        check_vma=False,
    )
```

profile of v0, /device:TPU:0, one launch (start us, length us, event | category | flops | bytes accessed | tf_op | source)
XLA Modules:
  0.0 302.8 jit_solution(8518955686776389047)
XLA Ops:
  2.3 1.9 multiply_convert_fusion.1
  4.6 7.5 %maximum_minimum_fusion = bf16[64,64,1024]{2,1,0:T(8,128)(2,1)} fusion(bf16[64,64,1024]{2,1,0:T(8,128)(2,1)} %param.21, bf16[64]{0:T(256)(128)(2,1)S(1)} %multiply_convert_fusion.2, bf16[64]{0:T(256)(128)(2,1)S(1)} %fusion.18), kind=kLoop, calls=%fused_computation.18 | loop fusion | flops 8388608 | bytes 16777472 | tf_op jit(solution)/shard_map/min | solution.py:66
  12.2 6.3 %fusion.2 = bf16[128,4096]{1,0:T(8,128)(2,1)S(1)} fusion(bf16[1024,128]{0,1:T(8,128)(2,1)S(1)} %convert_element_type.55, bf16[4096,1024]{1,0:T(8,128)(2,1)} %bitcast.198, f32[4096]{0:T(1024)S(1)} %select_n.40), kind=kOutput, calls=%fused_computation.20 | convolution fusion | flops 1074790400 | bytes 9715712 | tf_op jit(solution)/shard_map/dot_general | solution.py:69
  18.7 31.3 %all_to_all.5 = bf16[8,32,4096]{2,1,0:T(8,128)(2,1)S(1)} all-to-all(bf16[8,32,4096]{2,1,0:T(8,128)(2,1)S(1)} %bitcast.221), channel_id=1, replica_groups=mesh['z'=4,'ylo'=2,'x'=4,'yhi'=2,'core'=2] {'ylo','yhi','core'}, dimensions={0} | all-to-all | bytes 4194304 | tf_op jit(solution)/shard_map/all_to_all | solution.py:85
  50.0 5.5 %reshape.287 = bf16[2,4,16,2,64,64]{5,4,3,2,1,0:T(8,128)(2,1)} reshape(bf16[8,32,4096]{2,1,0:T(8,128)(2,1)S(1)} %all_to_all.5) | data formatting | bytes 4194304 | tf_op jit(solution)/shard_map/reshape | solution.py:86
  55.5 2.5 slice.64
  58.0 3.6 %copy.95 = bf16[9,2,2,64,4,64]{5,4,3,2,1,0:T(4,128)(2,1)} copy(bf16[9,2,2,64,4,64]{5,3,1,0,4,2:T(8,128)(2,1)S(1)} %slice.64) | data formatting | bytes 2359296 | tf_op jit(solution)/shard_map/slice | solution.py:93
  61.7 3.7 %slice.49 = bf16[9,2,128,256]{3,2,1,0:T(8,128)(2,1)S(1)} reshape(bf16[9,2,2,64,4,64]{5,4,3,2,1,0:T(4,128)(2,1)} %copy.95) | data formatting | bytes 2359296 | tf_op jit(solution)/shard_map/slice | solution.py:93
  65.4 2.8 collective-permute-start
  68.2 1.7 slice.67
  69.9 2.9 copy.96
  72.8 3.2 %slice.53 = bf16[7,2,128,256]{3,2,1,0:T(8,128)(2,1)S(1)} reshape(bf16[7,2,2,64,4,64]{5,4,3,2,1,0:T(4,128)(2,1)} %copy.96) | data formatting | bytes 1835008 | tf_op jit(solution)/shard_map/slice | solution.py:93
  76.0 4.1 %collective-permute-start.4 = (bf16[7,2,128,256]{3,2,1,0:T(8,128)(2,1)S(1)}, bf16[7,2,128,256]{3,2,1,0:T(8,128)(2,1)}, u32[]{:S(2)}, u32[]{:S(2)}) collective-permute-start(bf16[7,2,128,256]{3,2,1,0:T(8,128)(2,1)S(1)} %slice.53), channel_id=1, source_target_pairs={{32,0},{64,32},{96,64},{0,96},{33,1},{65,33},{97,65},{1,97},{34,2}... | collective-permute-start | bytes 2752520 | tf_op jit(solution)/shard_map/ppermute | solution.py:37
  80.4 18.8 %collective-permute-done.4 = bf16[7,2,128,256]{3,2,1,0:T(8,128)(2,1)} collective-permute-done((bf16[7,2,128,256]{3,2,1,0:T(8,128)(2,1)S(1)}, bf16[7,2,128,256]{3,2,1,0:T(8,128)(2,1)}, u32[]{:S(2)}, u32[]{:S(2)}) %collective-permute-start.4) | collective-permute-done | bytes 917536 | tf_op jit(solution)/shard_map/ppermute | solution.py:37
  100.3 3.9 %collective-permute-start.5 = (bf16[7,1,128,256]{3,2,1,0:T(8,128)(2,1)S(1)}, bf16[7,1,128,256]{3,2,1,0:T(8,128)(2,1)S(1)}, u32[]{:S(2)}, u32[]{:S(2)}) collective-permute-start(bf16[7,1,128,256]{3,2,1,0:T(8,128)(2,1)S(1)} %slice.68), channel_id=1, source_target_pairs={{32,0},{64,32},{96,64},{0,96},{33,1},{65,33},{97,65},{1,97},{34,2}... | collective-permute-start | bytes 1376264 | tf_op jit(solution)/shard_map/ppermute | solution.py:37
  106.3 3.0 collective-permute-start.1
  109.3 1.9 slice.66
  112.6 4.5 %collective-permute-done.7 = bf16[7,1,128,256]{3,2,1,0:T(8,128)(2,1)S(1)} collective-permute-done((bf16[7,1,128,256]{3,2,1,0:T(8,128)(2,1)S(1)}, bf16[7,1,128,256]{3,2,1,0:T(8,128)(2,1)S(1)}, u32[]{:S(2)}, u32[]{:S(2)}) %collective-permute-start.7) | collective-permute-done | bytes 458784 | tf_op jit(solution)/shard_map/ppermute | solution.py:37
  117.1 3.2 %conditional.5 = (bf16[4,7,2,128,256]{4,3,2,1,0:T(8,128)(2,1)}) conditional(s32[]{:T(128)} %clamp.8, (bf16[7,2,128,256]{3,2,1,0:T(8,128)(2,1)S(1)}, bf16[7,2,128,256]{3,2,1,0:T(8,128)(2,1)}, bf16[7,2,128,256]{3,2,1,0:T(8,128)(2,1)S(1)}, bf16[7,2,128,256]{3,2,1,0:T(8,128)(2,1)}) %tuple.62, ...), branch_computations={%region_5.6_spmd, %region_6.7_spmd, %region_7.8_spmd, %region_8.9_... | conditional | flops 5505024 | bytes 7340040 | solution.py:58
  117.2 3.2 %pad_maximum_fusion.4 = bf16[4,7,2,128,256]{4,3,2,1,0:T(8,128)(2,1)} fusion(bf16[1,7,2,128,256]{4,3,2,1,0:T(8,128)(2,1)} %bitcast.19, bf16[1,7,2,128,256]{4,3,2,1,0:T(8,128)(2,1)S(1)} %bitcast.213, bf16[1,7,2,128,256]{4,3,2,1,0:T(8,128)(2,1)} %bitcast.17, bf16[1,7,2,128,256]{4,3,2,1,0:T(8,128)(2,1)S(1)} %bitcast.199), kind=kLoop, calls=%fused_computation.4 | loop fusion | flops 5505024 | bytes 7340032 | tf_op jit(solution)/shard_map/cond/branch_0_fun/stack | solution.py:54
  120.4 1.1 constant_dynamic-update-slice_fusion.1
  121.5 4.1 %collective-permute-done.3 = bf16[9,1,128,256]{3,2,1,0:T(8,128)(2,1)} collective-permute-done((bf16[9,1,128,256]{3,2,1,0:T(8,128)(2,1)}, bf16[9,1,128,256]{3,2,1,0:T(8,128)(2,1)}, u32[]{:S(2)}, u32[]{:S(2)}) %collective-permute-start.3) | collective-permute-done | bytes 589856 | tf_op jit(solution)/shard_map/ppermute | solution.py:37
  126.7 3.8 %conditional.4 = (bf16[4,9,2,128,256]{4,3,2,1,0:T(8,128)(2,1)}) conditional(s32[]{:T(128)} %clamp.9, (bf16[9,2,128,256]{3,2,1,0:T(8,128)(2,1)S(1)}, bf16[9,2,128,256]{3,2,1,0:T(8,128)(2,1)}, bf16[9,2,128,256]{3,2,1,0:T(8,128)(2,1)S(1)}, bf16[9,2,128,256]{3,2,1,0:T(8,128)(2,1)}) %tuple.129, ...), branch_computations={%region_1.2_spmd, %region_2.3_spmd, %region_3.4_spmd, %region_4.5_... | conditional | flops 7077888 | bytes 9437192 | solution.py:58
  126.7 3.7 %pad_maximum_fusion = bf16[4,9,2,128,256]{4,3,2,1,0:T(8,128)(2,1)} fusion(bf16[1,9,2,128,256]{4,3,2,1,0:T(8,128)(2,1)} %bitcast.3, bf16[1,9,2,128,256]{4,3,2,1,0:T(8,128)(2,1)S(1)} %bitcast.207, bf16[1,9,2,128,256]{4,3,2,1,0:T(8,128)(2,1)} %bitcast.203, bf16[1,9,2,128,256]{4,3,2,1,0:T(8,128)(2,1)S(1)} %bitcast.194), kind=kLoop, calls=%fused_computation | loop fusion | flops 7077888 | bytes 9437184 | tf_op jit(solution)/shard_map/cond/branch_0_fun/stack | solution.py:54
  130.5 3.2 %collective-permute-start.8 = (bf16[4,9,2,128,256]{4,3,2,1,0:T(8,128)(2,1)}, bf16[4,9,2,128,256]{4,3,2,1,0:T(8,128)(2,1)S(1)}, u32[]{:S(2)}, u32[]{:S(2)}) collective-permute-start(bf16[4,9,2,128,256]{4,3,2,1,0:T(8,128)(2,1)} %get-tuple-element.255), channel_id=1, source_target_pairs={{32,0},{64,32},{96,64},{0,96},{33,1},{65,33},{97,65},{1,97},{34,2}... | collective-permute-start | bytes 14155784 | tf_op jit(solution)/shard_map/ppermute | solution.py:37
  133.7 3.2 %collective-permute-start.12 = (bf16[4,7,2,128,256]{4,3,2,1,0:T(8,128)(2,1)}, bf16[4,7,2,128,256]{4,3,2,1,0:T(8,128)(2,1)S(1)}, u32[]{:S(2)}, u32[]{:S(2)}) collective-permute-start(bf16[4,7,2,128,256]{4,3,2,1,0:T(8,128)(2,1)} %get-tuple-element.256), channel_id=1, source_target_pairs={{4,0},{8,4},{12,8},{0,12},{5,1},{9,5},{13,9},{1,13},{6,2},{10,6},{... | collective-permute-start | bytes 11010056 | tf_op jit(solution)/shard_map/ppermute | solution.py:37
  137.0 75.5 %collective-permute-done.14 = bf16[4,7,2,128,256]{4,3,2,1,0:T(8,128)(2,1)S(1)} collective-permute-done((bf16[4,7,2,128,256]{4,3,2,1,0:T(8,128)(2,1)}, bf16[4,7,2,128,256]{4,3,2,1,0:T(8,128)(2,1)S(1)}, u32[]{:S(2)}, u32[]{:S(2)}) %collective-permute-start.14) | collective-permute-done | bytes 3670048 | tf_op jit(solution)/shard_map/ppermute | solution.py:37
  212.5 1.4 slice.73
  213.9 1.5 slice.72
  215.3 3.2 %collective-permute-start.13 = (bf16[2,7,2,128,256]{4,3,2,1,0:T(8,128)(2,1)}, bf16[2,7,2,128,256]{4,3,2,1,0:T(8,128)(2,1)}, u32[]{:S(2)}, u32[]{:S(2)}) collective-permute-start(bf16[2,7,2,128,256]{4,3,2,1,0:T(8,128)(2,1)} %slice.72), channel_id=1, source_target_pairs={{4,0},{8,4},{12,8},{0,12},{5,1},{9,5},{13,9},{1,13},{6,2},{10,6},{... | collective-permute-start | bytes 5505032 | tf_op jit(solution)/shard_map/ppermute | solution.py:37
  219.3 13.0 %collective-permute-done.10 = bf16[4,9,2,128,256]{4,3,2,1,0:T(8,128)(2,1)S(1)} collective-permute-done((bf16[4,9,2,128,256]{4,3,2,1,0:T(8,128)(2,1)}, bf16[4,9,2,128,256]{4,3,2,1,0:T(8,128)(2,1)S(1)}, u32[]{:S(2)}, u32[]{:S(2)}) %collective-permute-start.10) | collective-permute-done | bytes 4718624 | tf_op jit(solution)/shard_map/ppermute | solution.py:37
  232.3 1.6 slice.71
  233.9 1.6 slice.70
  235.5 3.2 %collective-permute-start.9 = (bf16[2,9,2,128,256]{4,3,2,1,0:T(8,128)(2,1)}, bf16[2,9,2,128,256]{4,3,2,1,0:T(8,128)(2,1)}, u32[]{:S(2)}, u32[]{:S(2)}) collective-permute-start(bf16[2,9,2,128,256]{4,3,2,1,0:T(8,128)(2,1)} %slice.70), channel_id=1, source_target_pairs={{32,0},{64,32},{96,64},{0,96},{33,1},{65,33},{97,65},{1,97},{34,2}... | collective-permute-start | bytes 7077896 | tf_op jit(solution)/shard_map/ppermute | solution.py:37
  238.7 1.6 convolution_bitcast_fusion.3
  241.4 1.6 copy-done.6
  244.7 3.0 %convolution_bitcast_fusion = f32[9,2,64,512]{3,2,1,0:T(8,128)} fusion(bf16[9,2,512,256,1]{3,2,1,4,0:T(8,128)(2,1)S(1)} %bitcast.191, bf16[9,2,64,2,256]{4,2,0,3,1:T(8,128)(2,1)S(1)} %pad_maximum_fusion.18), kind=kOutput, calls=%fused_computation.24 | convolution fusion | flops 603979776 | bytes 8257536 | tf_op jit(solution)/shard_map/fqipw,fpjw->fqij/dot_general | solution.py:107
  247.8 3.0 convolution_bitcast_fusion.2
  250.8 1.7 collective-permute-done.15
  253.2 2.4 pad_maximum_fusion.17
  255.8 20.0 %conditional.6 = (bf16[7,2,2048,256]{3,2,1,0:T(8,128)(2,1)}) conditional(s32[]{:T(128)} %clamp.9, (bf16[7,2,4,2,64,256]{5,4,3,2,1,0:T(8,128)(2,1)S(1)}, bf16[7,2,4,2,64,256]{5,4,3,2,1,0:T(8,128)(2,1)S(1)}, bf16[7,2,4,2,64,256]{5,4,3,2,1,0:T(8,128)(2,1)S(1)}, bf16[7,2,4,2,64,256]{5,4,3,2,1,0:T(8,128)(2,1)S(1)}) %tuple.117, ...), branch_computations={%region_9.10_spmd, %region_10.11_spmd, %region_11.12_spmd, %region... | conditional | flops 22020096 | bytes 58720264 | solution.py:58
  255.8 6.5 %pad_maximum_fusion.8 = bf16[7,2,4,2,4,64,256]{6,5,3,2,1,0,4:T(8,128)(2,1)} fusion(bf16[7,2,4,2,1,64,256]{6,5,3,2,1,0,4:T(8,128)(2,1)S(1)} %bitcast.166, bf16[7,2,4,2,1,64,256]{6,5,3,2,1,0,4:T(8,128)(2,1)S(1)} %bitcast.182, bf16[7,2,4,2,1,64,256]{6,5,3,2,1,0,4:T(8,128)(2,1)S(1)} %bitcast.174, bf16[7,2,4,2,1,64,256]{6,5,3,2,1,0,4:T(8,128)(2,1)S(1)} %bitcast.158), kind=kLoop, calls=%fused_computation.8 | loop fusion | flops 22020096 | bytes 29360128 | tf_op jit(solution)/shard_map/cond/branch_0_fun/stack | solution.py:54
  262.3 13.5 %copy.90 = bf16[7,2,4,2,4,64,256]{6,5,4,3,2,1,0:T(8,128)(2,1)} copy(bf16[7,2,4,2,4,64,256]{6,5,3,2,1,0,4:T(8,128)(2,1)} %pad_maximum_fusion.8) | data formatting | bytes 29360128 | tf_op jit(solution)/shard_map/cond/branch_0_fun/stack | solution.py:54
  275.8 13.2 %fusion.3 = f32[7,2,64,2048]{3,2,1,0:T(8,128)} fusion(bf16[7,2,2048,256]{3,2,1,0:T(8,128)(2,1)} %get-tuple-element.257, bf16[7,2,64,2,256]{4,2,0,3,1:T(8,128)(2,1)} %pad_maximum_fusion.19), kind=kOutput, calls=%fused_computation.22 | convolution fusion | flops 1879048192 | bytes 22937600 | tf_op jit(solution)/shard_map/fqipw,fpjw->fqij/dot_general | solution.py:112
  289.0 2.8 pad_maximum_fusion.16
  292.5 1.6 convolution_bitcast_fusion.1
  296.5 6.4 %conditional.7 = (f32[16,2,64,2048]{3,2,1,0:T(8,128)}) conditional(s32[]{:T(128)} %clamp.8, (f32[9,2,64,512]{3,2,1,0:T(8,128)S(1)}, f32[9,2,64,512]{3,2,1,0:T(8,128)S(1)}, f32[9,2,64,512]{3,2,1,0:T(8,128)S(1)}, f32[9,2,64,512]{3,2,1,0:T(8,128)S(1)}, f32[7,2,64,2048]{3,2,1,0:T(8,128)S(1)}) %tuple.125, ...), branch_computations={%region_13.14_spmd, %region_14.15_spmd, %region_15.16_spmd, %regio... | conditional | flops 16777216 | bytes 33554440 | solution.py:124
  296.5 6.4 %pad_maximum_fusion.12 = f32[16,2,64,2048]{3,2,1,0:T(8,128)} fusion(f32[7,2,64,2048]{3,2,1,0:T(8,128)S(1)} %get-tuple-element.214, f32[9,2,64,512]{3,2,1,0:T(8,128)S(1)} %get-tuple-element.213, f32[9,2,64,512]{3,2,1,0:T(8,128)S(1)} %get-tuple-element.212, f32[9,2,64,512]{3,2,1,0:T(8,128)S(1)} %get-tuple-element.211, f32[9,2,64,512]{3,2,1,0:T(8,128)S(1)} %get-tuple-element.210), kind=kLoop, calls=%fused_computation.12 | loop fusion | flops 16777216 | bytes 33554432 | tf_op jit(solution)/shard_map/cond/branch_0_fun/concatenate | solution.py:119
  (70 shorter events, 16.3 us)
Async XLA Ops:
  65.4 39.9 %collective-permute-start = (bf16[9,2,128,256]{3,2,1,0:T(8,128)(2,1)S(1)}, bf16[9,2,128,256]{3,2,1,0:T(8,128)(2,1)S(1)}, u32[]{:S(2)}, u32[]{:S(2)}) collective-permute-start(bf16[9,2,128,256]{3,2,1,0:T(8,128)(2,1)S(1)} %slice.49), channel_id=1, source_target_pairs={{4,0},{8,4},{12,8},{0,12},{5,1},{9,5},{13,9},{1,13},{6,2},{10,6},{... | collective-permute-start | bytes 3538952 | tf_op jit(solution)/shard_map/ppermute | solution.py:37
  68.2 41.1 %collective-permute-start.2 = (bf16[9,2,128,256]{3,2,1,0:T(8,128)(2,1)S(1)}, bf16[9,2,128,256]{3,2,1,0:T(8,128)(2,1)}, u32[]{:S(2)}, u32[]{:S(2)}) collective-permute-start(bf16[9,2,128,256]{3,2,1,0:T(8,128)(2,1)S(1)} %slice.49), channel_id=1, source_target_pairs={{12,0},{0,4},{4,8},{8,12},{13,1},{1,5},{5,9},{9,13},{14,2},{2,6},{... | collective-permute-start | bytes 3538952 | tf_op jit(solution)/shard_map/ppermute | solution.py:37
  76.0 23.2 %collective-permute-start.4 = (bf16[7,2,128,256]{3,2,1,0:T(8,128)(2,1)S(1)}, bf16[7,2,128,256]{3,2,1,0:T(8,128)(2,1)}, u32[]{:S(2)}, u32[]{:S(2)}) collective-permute-start(bf16[7,2,128,256]{3,2,1,0:T(8,128)(2,1)S(1)} %slice.53), channel_id=1, source_target_pairs={{32,0},{64,32},{96,64},{0,96},{33,1},{65,33},{97,65},{1,97},{34,2}... | collective-permute-start | bytes 2752520 | tf_op jit(solution)/shard_map/ppermute | solution.py:37
  80.1 24.1 %collective-permute-start.6 = (bf16[7,2,128,256]{3,2,1,0:T(8,128)(2,1)S(1)}, bf16[7,2,128,256]{3,2,1,0:T(8,128)(2,1)}, u32[]{:S(2)}, u32[]{:S(2)}) collective-permute-start(bf16[7,2,128,256]{3,2,1,0:T(8,128)(2,1)S(1)} %slice.53), channel_id=1, source_target_pairs={{96,0},{0,32},{32,64},{64,96},{97,1},{1,33},{33,65},{65,97},{98,2}... | collective-permute-start | bytes 2752520 | tf_op jit(solution)/shard_map/ppermute | solution.py:37
  100.3 12.2 %collective-permute-start.5 = (bf16[7,1,128,256]{3,2,1,0:T(8,128)(2,1)S(1)}, bf16[7,1,128,256]{3,2,1,0:T(8,128)(2,1)S(1)}, u32[]{:S(2)}, u32[]{:S(2)}) collective-permute-start(bf16[7,1,128,256]{3,2,1,0:T(8,128)(2,1)S(1)} %slice.68), channel_id=1, source_target_pairs={{32,0},{64,32},{96,64},{0,96},{33,1},{65,33},{97,65},{1,97},{34,2}... | collective-permute-start | bytes 1376264 | tf_op jit(solution)/shard_map/ppermute | solution.py:37
  105.2 11.9 %collective-permute-start.7 = (bf16[7,1,128,256]{3,2,1,0:T(8,128)(2,1)S(1)}, bf16[7,1,128,256]{3,2,1,0:T(8,128)(2,1)S(1)}, u32[]{:S(2)}, u32[]{:S(2)}) collective-permute-start(bf16[7,1,128,256]{3,2,1,0:T(8,128)(2,1)S(1)} %slice.69), channel_id=1, source_target_pairs={{96,0},{0,32},{32,64},{64,96},{97,1},{1,33},{33,65},{65,97},{98,2}... | collective-permute-start | bytes 1376264 | tf_op jit(solution)/shard_map/ppermute | solution.py:37
  105.3 7.0 %copy-start.2 = (bf16[9,2,128,256]{3,2,1,0:T(8,128)(2,1)}, bf16[9,2,128,256]{3,2,1,0:T(8,128)(2,1)S(1)}, u32[]{:S(2)}) copy-start(bf16[9,2,128,256]{3,2,1,0:T(8,128)(2,1)S(1)} %collective-permute-done) | copy-start | bytes 3538948
  106.3 14.1 %collective-permute-start.1 = (bf16[9,1,128,256]{3,2,1,0:T(8,128)(2,1)}, bf16[9,1,128,256]{3,2,1,0:T(8,128)(2,1)}, u32[]{:S(2)}, u32[]{:S(2)}) collective-permute-start(bf16[9,1,128,256]{3,2,1,0:T(8,128)(2,1)} %slice.65), channel_id=1, source_target_pairs={{4,0},{8,4},{12,8},{0,12},{5,1},{9,5},{13,9},{1,13},{6,2},{10,6},{... | collective-permute-start | bytes 1769480 | tf_op jit(solution)/shard_map/ppermute | solution.py:37
  111.3 14.3 %collective-permute-start.3 = (bf16[9,1,128,256]{3,2,1,0:T(8,128)(2,1)}, bf16[9,1,128,256]{3,2,1,0:T(8,128)(2,1)}, u32[]{:S(2)}, u32[]{:S(2)}) collective-permute-start(bf16[9,1,128,256]{3,2,1,0:T(8,128)(2,1)} %slice.66), channel_id=1, source_target_pairs={{12,0},{0,4},{4,8},{8,12},{13,1},{1,5},{5,9},{9,13},{14,2},{2,6},{... | collective-permute-start | bytes 1769480 | tf_op jit(solution)/shard_map/ppermute | solution.py:37
  130.5 88.1 %copy-start.3 = (bf16[4,9,2,128,256]{4,3,2,1,0:T(8,128)(2,1)S(1)}, bf16[4,9,2,128,256]{4,3,2,1,0:T(8,128)(2,1)}, u32[]{:S(2)}) copy-start(bf16[4,9,2,128,256]{4,3,2,1,0:T(8,128)(2,1)} %get-tuple-element.255) | copy-start | bytes 14155780
  130.5 101.8 %collective-permute-start.10 = (bf16[4,9,2,128,256]{4,3,2,1,0:T(8,128)(2,1)}, bf16[4,9,2,128,256]{4,3,2,1,0:T(8,128)(2,1)S(1)}, u32[]{:S(2)}, u32[]{:S(2)}) collective-permute-start(bf16[4,9,2,128,256]{4,3,2,1,0:T(8,128)(2,1)} %get-tuple-element.255), channel_id=1, source_target_pairs={{96,0},{0,32},{32,64},{64,96},{97,1},{1,33},{33,65},{65,97},{98,2}... | collective-permute-start | bytes 14155784 | tf_op jit(solution)/shard_map/ppermute | solution.py:37
  130.5 103.4 %collective-permute-start.8 = (bf16[4,9,2,128,256]{4,3,2,1,0:T(8,128)(2,1)}, bf16[4,9,2,128,256]{4,3,2,1,0:T(8,128)(2,1)S(1)}, u32[]{:S(2)}, u32[]{:S(2)}) collective-permute-start(bf16[4,9,2,128,256]{4,3,2,1,0:T(8,128)(2,1)} %get-tuple-element.255), channel_id=1, source_target_pairs={{32,0},{64,32},{96,64},{0,96},{33,1},{65,33},{97,65},{1,97},{34,2}... | collective-permute-start | bytes 14155784 | tf_op jit(solution)/shard_map/ppermute | solution.py:37
  133.7 78.8 %collective-permute-start.14 = (bf16[4,7,2,128,256]{4,3,2,1,0:T(8,128)(2,1)}, bf16[4,7,2,128,256]{4,3,2,1,0:T(8,128)(2,1)S(1)}, u32[]{:S(2)}, u32[]{:S(2)}) collective-permute-start(bf16[4,7,2,128,256]{4,3,2,1,0:T(8,128)(2,1)} %get-tuple-element.256), channel_id=1, source_target_pairs={{12,0},{0,4},{4,8},{8,12},{13,1},{1,5},{5,9},{9,13},{14,2},{2,6},{... | collective-permute-start | bytes 11010056 | tf_op jit(solution)/shard_map/ppermute | solution.py:37
  133.7 80.1 %collective-permute-start.12 = (bf16[4,7,2,128,256]{4,3,2,1,0:T(8,128)(2,1)}, bf16[4,7,2,128,256]{4,3,2,1,0:T(8,128)(2,1)S(1)}, u32[]{:S(2)}, u32[]{:S(2)}) collective-permute-start(bf16[4,7,2,128,256]{4,3,2,1,0:T(8,128)(2,1)} %get-tuple-element.256), channel_id=1, source_target_pairs={{4,0},{8,4},{12,8},{0,12},{5,1},{9,5},{13,9},{1,13},{6,2},{10,6},{... | collective-permute-start | bytes 11010056 | tf_op jit(solution)/shard_map/ppermute | solution.py:37
  213.8 38.6 %collective-permute-start.15 = (bf16[2,7,2,128,256]{4,3,2,1,0:T(8,128)(2,1)}, bf16[2,7,2,128,256]{4,3,2,1,0:T(8,128)(2,1)}, u32[]{:S(2)}, u32[]{:S(2)}) collective-permute-start(bf16[2,7,2,128,256]{4,3,2,1,0:T(8,128)(2,1)} %slice.73), channel_id=1, source_target_pairs={{12,0},{0,4},{4,8},{8,12},{13,1},{1,5},{5,9},{9,13},{14,2},{2,6},{... | collective-permute-start | bytes 5505032 | tf_op jit(solution)/shard_map/ppermute | solution.py:37
  213.9 4.7 %copy-start.5 = (bf16[4,7,2,128,256]{4,3,2,1,0:T(8,128)(2,1)}, bf16[4,7,2,128,256]{4,3,2,1,0:T(8,128)(2,1)S(1)}, u32[]{:S(2)}) copy-start(bf16[4,7,2,128,256]{4,3,2,1,0:T(8,128)(2,1)S(1)} %collective-permute-done.12) | copy-start | bytes 11010052
  215.3 37.9 %collective-permute-start.13 = (bf16[2,7,2,128,256]{4,3,2,1,0:T(8,128)(2,1)}, bf16[2,7,2,128,256]{4,3,2,1,0:T(8,128)(2,1)}, u32[]{:S(2)}, u32[]{:S(2)}) collective-permute-start(bf16[2,7,2,128,256]{4,3,2,1,0:T(8,128)(2,1)} %slice.72), channel_id=1, source_target_pairs={{4,0},{8,4},{12,8},{0,12},{5,1},{9,5},{13,9},{1,13},{6,2},{10,6},{... | collective-permute-start | bytes 5505032 | tf_op jit(solution)/shard_map/ppermute | solution.py:37
  233.8 55.1 %collective-permute-start.11 = (bf16[2,9,2,128,256]{4,3,2,1,0:T(8,128)(2,1)}, bf16[2,9,2,128,256]{4,3,2,1,0:T(8,128)(2,1)}, u32[]{:S(2)}, u32[]{:S(2)}) collective-permute-start(bf16[2,9,2,128,256]{4,3,2,1,0:T(8,128)(2,1)} %slice.71), channel_id=1, source_target_pairs={{96,0},{0,32},{32,64},{64,96},{97,1},{1,33},{33,65},{65,97},{98,2}... | collective-permute-start | bytes 7077896 | tf_op jit(solution)/shard_map/ppermute | solution.py:37
  235.5 53.5 %collective-permute-start.9 = (bf16[2,9,2,128,256]{4,3,2,1,0:T(8,128)(2,1)}, bf16[2,9,2,128,256]{4,3,2,1,0:T(8,128)(2,1)}, u32[]{:S(2)}, u32[]{:S(2)}) collective-permute-start(bf16[2,9,2,128,256]{4,3,2,1,0:T(8,128)(2,1)} %slice.70), channel_id=1, source_target_pairs={{32,0},{64,32},{96,64},{0,96},{33,1},{65,33},{97,65},{1,97},{34,2}... | collective-permute-start | bytes 7077896 | tf_op jit(solution)/shard_map/ppermute | solution.py:37
  238.7 2.0 copy-start.4
  241.0 2.0 copy-start.6
  291.8 2.4 slice-start
  292.5 2.6 slice-start.1
  292.5 3.3 %copy-start = (f32[9,2,64,512]{3,2,1,0:T(8,128)S(1)}, f32[9,2,64,512]{3,2,1,0:T(8,128)}, u32[]{:S(2)}) copy-start(f32[9,2,64,512]{3,2,1,0:T(8,128)} %convolution_bitcast_fusion) | copy-start | bytes 7077892
  292.5 3.9 %copy-start.1 = (f32[9,2,64,512]{3,2,1,0:T(8,128)S(1)}, f32[9,2,64,512]{3,2,1,0:T(8,128)}, u32[]{:S(2)}) copy-start(f32[9,2,64,512]{3,2,1,0:T(8,128)} %convolution_bitcast_fusion.2) | copy-start | bytes 7077892
where the time goes:
time: 305 us; the launch traced here: 303 us
  waiting for transfers between devices  119 us (39%)
  local copies, waits for them, and re-layouts  58.9 us (19%)
  other arithmetic  38.2 us (13%)
  blocking collectives  31.3 us (10%)
  matrix products  28.8 us (9%)
  starting transfers between devices  26.8 us (9%)
    ppermute x16, waiting for transfers between devices, shifted(): lax.ppermute(block, axis, [((i + distance) % size, i) for i in range(size)])  119 us
    all_to_all x1, blocking collectives, per_device(): lax.all_to_all(outgoing, ('ylo', 'yhi', 'core'), 0, 0, tiled=True)  31.3 us
    ppermute x16, starting transfers between devices, shifted(): lax.ppermute(block, axis, [((i + distance) % size, i) for i in range(size)])  26.8 us
    slice x6, local copies, waits for them, and re-layouts, per_device(): low, high = (panel[:split], panel[split:])  17.7 us
    another operation x1, local copies, waits for them, and re-layouts, arrangement(): jnp.stack([blocks[(k - at) % size] for k in range(size)], axis=stack_axis)  13.5 us
    another operation x3, other arithmetic, arrangement(): jnp.stack([blocks[(k - at) % size] for k in range(size)], axis=stack_axis)  13.5 us
    dot_general x1, matrix products, per_device(): jnp.einsum('fqipw,fpjw->fqij', rows_high, second, preferred_element_type=...  13.2 us
    dot_general x4, matrix products, products(): jnp.einsum('fqipw,fpjw->fqij', part, block, preferred_element_type=jnp.fl...  9.33 us
  transfers between devices with their start and end apart: 16, of which 8 were waited for; matrix products, arithmetic and copies ran while one was open for 23% of the time, Pallas kernels for 0%

commit v1 on v0

--- a/solution.py
+++ b/solution.py
@@ -96,9 +96,8 @@
     at = lax.axis_index("ylo") * channels
     rows_low = row_operand(lax.dynamic_slice_in_dim(low, at, channels, axis=2))
     rows_high = row_operand(lax.dynamic_slice_in_dim(high, at, channels, axis=2))
-    first, second, rows_low, rows_high = lax.optimization_barrier(
-        (first, second, rows_low, rows_high)
-    )
+    first, rows_low = lax.optimization_barrier((first, rows_low))
+    second, rows_high = lax.optimization_barrier((second, rows_high))
     shape = (xs, -1, 2, pairs, channels, groups * win_local)
     width = pairs * channels * xs
 

time: 305 us -> 300 us (0.984)
  waiting for transfers between devices: 119 us -> 108 us
  local copies, waits for them, and re-layouts: 58.9 us -> 66.4 us
    ppermute x16, waiting for transfers between devices: 119 us -> 108 us  [shifted(): lax.ppermute(block, axis, [((i + distance) % size, i) for i in range(size)])]
    reshape x3, local copies, waits for them, and re-layouts: 2.14 us -> 6.14 us  [products(): block.reshape(shape)]
  transfers between devices with their start and end apart: 16 -> 16, of which waited for: 8 -> 8; matrix products, arithmetic and copies ran while one was open for 23% -> 28% of each run, Pallas kernels for 0% -> 0%
where the time goes in v1:
time: 300 us; the launch traced here: 299 us
  waiting for transfers between devices  108 us (36%)
  local copies, waits for them, and re-layouts  66.4 us (22%)
  other arithmetic  37.8 us (13%)
  blocking collectives  31.3 us (10%)
  matrix products  28.8 us (10%)
  starting transfers between devices  26.4 us (9%)
    ppermute x16, waiting for transfers between devices, shifted(): lax.ppermute(block, axis, [((i + distance) % size, i) for i in range(size)])  108 us
    all_to_all x1, blocking collectives, per_device(): lax.all_to_all(outgoing, ('ylo', 'yhi', 'core'), 0, 0, tiled=True)  31.3 us
    ppermute x16, starting transfers between devices, shifted(): lax.ppermute(block, axis, [((i + distance) % size, i) for i in range(size)])  26.4 us
    slice x6, local copies, waits for them, and re-layouts, per_device(): low, high = (panel[:split], panel[split:])  17.7 us
    another operation x1, local copies, waits for them, and re-layouts, arrangement(): jnp.stack([blocks[(k - at) % size] for k in range(size)], axis=stack_axis)  13.5 us
    another operation x3, other arithmetic, arrangement(): jnp.stack([blocks[(k - at) % size] for k in range(size)], axis=stack_axis)  13.4 us
    dot_general x1, matrix products, per_device(): jnp.einsum('fqipw,fpjw->fqij', rows_high, second, preferred_element_type=...  13.2 us
    dot_general x4, matrix products, products(): jnp.einsum('fqipw,fpjw->fqij', part, block, preferred_element_type=jnp.fl...  9.31 us
  transfers between devices with their start and end apart: 16, of which 8 were waited for; matrix products, arithmetic and copies ran while one was open for 28% of the time, Pallas kernels for 0%

profile of v1, /device:TPU:0, one launch (start us, length us, event | category | flops | bytes accessed | tf_op | source)
XLA Modules:
  0.0 299.4 jit_solution(2157867743624882249)
XLA Ops:
  2.3 1.9 multiply_convert_fusion.1
  4.7 7.5 %maximum_minimum_fusion = bf16[64,64,1024]{2,1,0:T(8,128)(2,1)} fusion(bf16[64,64,1024]{2,1,0:T(8,128)(2,1)} %param.21, bf16[64]{0:T(256)(128)(2,1)S(1)} %multiply_convert_fusion.2, bf16[64]{0:T(256)(128)(2,1)S(1)} %fusion.18), kind=kLoop, calls=%fused_computation.18 | loop fusion | flops 8388608 | bytes 16777472 | tf_op jit(solution)/shard_map/min | solution.py:66
  12.2 6.3 %fusion.2 = bf16[128,4096]{1,0:T(8,128)(2,1)S(1)} fusion(bf16[1024,128]{0,1:T(8,128)(2,1)S(1)} %convert_element_type.55, bf16[4096,1024]{1,0:T(8,128)(2,1)} %bitcast.198, f32[4096]{0:T(1024)S(1)} %select_n.40), kind=kOutput, calls=%fused_computation.20 | convolution fusion | flops 1074790400 | bytes 9715712 | tf_op jit(solution)/shard_map/dot_general | solution.py:69
  18.7 31.3 %all_to_all.5 = bf16[8,32,4096]{2,1,0:T(8,128)(2,1)S(1)} all-to-all(bf16[8,32,4096]{2,1,0:T(8,128)(2,1)S(1)} %bitcast.219), channel_id=1, replica_groups=mesh['z'=4,'ylo'=2,'x'=4,'yhi'=2,'core'=2] {'ylo','yhi','core'}, dimensions={0} | all-to-all | bytes 4194304 | tf_op jit(solution)/shard_map/all_to_all | solution.py:85
  50.0 5.5 %reshape.287 = bf16[2,4,16,2,64,64]{5,4,3,2,1,0:T(8,128)(2,1)} reshape(bf16[8,32,4096]{2,1,0:T(8,128)(2,1)S(1)} %all_to_all.5) | data formatting | bytes 4194304 | tf_op jit(solution)/shard_map/reshape | solution.py:86
  55.5 2.5 slice.64
  58.0 3.7 %copy.95 = bf16[9,2,2,64,4,64]{5,4,3,2,1,0:T(4,128)(2,1)} copy(bf16[9,2,2,64,4,64]{5,3,1,0,4,2:T(8,128)(2,1)S(1)} %slice.64) | data formatting | bytes 2359296 | tf_op jit(solution)/shard_map/slice | solution.py:93
  61.7 3.7 %slice.49 = bf16[9,2,128,256]{3,2,1,0:T(8,128)(2,1)S(1)} reshape(bf16[9,2,2,64,4,64]{5,4,3,2,1,0:T(4,128)(2,1)} %copy.95) | data formatting | bytes 2359296 | tf_op jit(solution)/shard_map/slice | solution.py:93
  65.4 2.8 collective-permute-start
  68.3 1.7 slice.69
  69.9 2.9 copy.105
  72.9 3.2 %slice.57 = bf16[7,2,128,256]{3,2,1,0:T(8,128)(2,1)S(1)} reshape(bf16[7,2,2,64,4,64]{5,4,3,2,1,0:T(4,128)(2,1)} %copy.105) | data formatting | bytes 1835008 | tf_op jit(solution)/shard_map/slice | solution.py:93
  76.0 4.1 %collective-permute-start.8 = (bf16[7,2,128,256]{3,2,1,0:T(8,128)(2,1)S(1)}, bf16[7,2,128,256]{3,2,1,0:T(8,128)(2,1)}, u32[]{:S(2)}, u32[]{:S(2)}) collective-permute-start(bf16[7,2,128,256]{3,2,1,0:T(8,128)(2,1)S(1)} %slice.57), channel_id=1, source_target_pairs={{32,0},{64,32},{96,64},{0,96},{33,1},{65,33},{97,65},{1,97},{34,2}... | collective-permute-start | bytes 2752520 | tf_op jit(solution)/shard_map/ppermute | solution.py:37
  81.0 12.3 %collective-permute-done = bf16[9,2,128,256]{3,2,1,0:T(8,128)(2,1)S(1)} collective-permute-done((bf16[9,2,128,256]{3,2,1,0:T(8,128)(2,1)S(1)}, bf16[9,2,128,256]{3,2,1,0:T(8,128)(2,1)S(1)}, u32[]{:S(2)}, u32[]{:S(2)}) %collective-permute-start) | collective-permute-done | bytes 1179680 | tf_op jit(solution)/shard_map/ppermute | solution.py:37
  93.3 3.8 %collective-permute-start.1 = (bf16[9,1,128,256]{3,2,1,0:T(8,128)(2,1)S(1)}, bf16[9,1,128,256]{3,2,1,0:T(8,128)(2,1)S(1)}, u32[]{:S(2)}, u32[]{:S(2)}) collective-permute-start(bf16[9,1,128,256]{3,2,1,0:T(8,128)(2,1)S(1)} %slice.65), channel_id=1, source_target_pairs={{4,0},{8,4},{12,8},{0,12},{5,1},{9,5},{13,9},{1,13},{6,2},{10,6},{... | collective-permute-start | bytes 1769480 | tf_op jit(solution)/shard_map/ppermute | solution.py:37
  99.3 1.8 slice.70
  101.1 3.8 %collective-permute-start.9 = (bf16[7,1,128,256]{3,2,1,0:T(8,128)(2,1)}, bf16[7,1,128,256]{3,2,1,0:T(8,128)(2,1)}, u32[]{:S(2)}, u32[]{:S(2)}) collective-permute-start(bf16[7,1,128,256]{3,2,1,0:T(8,128)(2,1)} %slice.70), channel_id=1, source_target_pairs={{32,0},{64,32},{96,64},{0,96},{33,1},{65,33},{97,65},{1,97},{34,2}... | collective-permute-start | bytes 1376264 | tf_op jit(solution)/shard_map/ppermute | solution.py:37
  104.9 1.8 slice.71
  106.7 2.0 collective-permute-done.1
  108.7 4.6 %collective-permute-done.3 = bf16[9,1,128,256]{3,2,1,0:T(8,128)(2,1)S(1)} collective-permute-done((bf16[9,1,128,256]{3,2,1,0:T(8,128)(2,1)S(1)}, bf16[9,1,128,256]{3,2,1,0:T(8,128)(2,1)S(1)}, u32[]{:S(2)}, u32[]{:S(2)}) %collective-permute-start.3) | collective-permute-done | bytes 589856 | tf_op jit(solution)/shard_map/ppermute | solution.py:37
  113.4 3.6 %conditional.4 = (bf16[4,9,2,128,256]{4,3,2,1,0:T(8,128)(2,1)}) conditional(s32[]{:T(128)} %clamp.9, (bf16[9,2,128,256]{3,2,1,0:T(8,128)(2,1)S(1)}, bf16[9,2,128,256]{3,2,1,0:T(8,128)(2,1)S(1)}, bf16[9,2,128,256]{3,2,1,0:T(8,128)(2,1)S(1)}, bf16[9,2,128,256]{3,2,1,0:T(8,128)(2,1)}) %tuple.131, ...), branch_computations={%region_1.2_spmd, %region_2.3_spmd, %region_3.4_spmd, %region_4.5_... | conditional | flops 7077888 | bytes 9437192 | solution.py:58
  113.4 3.6 %pad_maximum_fusion = bf16[4,9,2,128,256]{4,3,2,1,0:T(8,128)(2,1)} fusion(bf16[1,9,2,128,256]{4,3,2,1,0:T(8,128)(2,1)} %bitcast.3, bf16[1,9,2,128,256]{4,3,2,1,0:T(8,128)(2,1)S(1)} %bitcast.207, bf16[1,9,2,128,256]{4,3,2,1,0:T(8,128)(2,1)S(1)} %bitcast.203, bf16[1,9,2,128,256]{4,3,2,1,0:T(8,128)(2,1)S(1)} %bitcast.194), kind=kLoop, calls=%fused_computation | loop fusion | flops 7077888 | bytes 9437184 | tf_op jit(solution)/shard_map/cond/branch_0_fun/stack | solution.py:54
  117.0 1.8 collective-permute-start.6
  118.8 2.2 collective-permute-start.4
  125.3 3.4 %conditional.5 = (bf16[4,7,2,128,256]{4,3,2,1,0:T(8,128)(2,1)}) conditional(s32[]{:T(128)} %clamp.8, (bf16[7,2,128,256]{3,2,1,0:T(8,128)(2,1)S(1)}, bf16[7,2,128,256]{3,2,1,0:T(8,128)(2,1)}, bf16[7,2,128,256]{3,2,1,0:T(8,128)(2,1)S(1)}, bf16[7,2,128,256]{3,2,1,0:T(8,128)(2,1)}) %tuple.64, ...), branch_computations={%region_5.6_spmd, %region_6.7_spmd, %region_7.8_spmd, %region_8.9_... | conditional | flops 5505024 | bytes 7340040 | solution.py:58
  125.3 3.3 %pad_maximum_fusion.4 = bf16[4,7,2,128,256]{4,3,2,1,0:T(8,128)(2,1)} fusion(bf16[1,7,2,128,256]{4,3,2,1,0:T(8,128)(2,1)} %bitcast.19, bf16[1,7,2,128,256]{4,3,2,1,0:T(8,128)(2,1)S(1)} %bitcast.213, bf16[1,7,2,128,256]{4,3,2,1,0:T(8,128)(2,1)} %bitcast.17, bf16[1,7,2,128,256]{4,3,2,1,0:T(8,128)(2,1)S(1)} %bitcast.199), kind=kLoop, calls=%fused_computation.4 | loop fusion | flops 5505024 | bytes 7340032 | tf_op jit(solution)/shard_map/cond/branch_0_fun/stack | solution.py:54
  128.7 2.0 collective-permute-start.14
  130.7 76.9 %collective-permute-done.12 = bf16[4,7,2,128,256]{4,3,2,1,0:T(8,128)(2,1)S(1)} collective-permute-done((bf16[4,7,2,128,256]{4,3,2,1,0:T(8,128)(2,1)}, bf16[4,7,2,128,256]{4,3,2,1,0:T(8,128)(2,1)S(1)}, u32[]{:S(2)}, u32[]{:S(2)}) %collective-permute-start.12) | collective-permute-done | bytes 3670048 | tf_op jit(solution)/shard_map/ppermute | solution.py:37
  212.6 2.7 copy.97
  215.3 5.0 %collective-permute-done.4 = bf16[4,9,2,128,256]{4,3,2,1,0:T(8,128)(2,1)} collective-permute-done((bf16[4,9,2,128,256]{4,3,2,1,0:T(8,128)(2,1)}, bf16[4,9,2,128,256]{4,3,2,1,0:T(8,128)(2,1)}, u32[]{:S(2)}, u32[]{:S(2)}) %collective-permute-start.4) | collective-permute-done | bytes 4718624 | tf_op jit(solution)/shard_map/ppermute | solution.py:37
  220.3 3.4 %slice.67 = bf16[2,9,2,128,256]{4,3,2,1,0:T(8,128)(2,1)} slice(bf16[4,9,2,128,256]{4,3,2,1,0:T(8,128)(2,1)} %collective-permute-done.4), slice={[0:2], [0:9], [0:2], [0:128], [0:256]} | slice | bytes 4718592 | tf_op jit(solution)/shard_map/slice | solution.py:44
  223.7 3.7 %collective-permute-start.5 = (bf16[2,9,2,128,256]{4,3,2,1,0:T(8,128)(2,1)}, bf16[2,9,2,128,256]{4,3,2,1,0:T(8,128)(2,1)}, u32[]{:S(2)}, u32[]{:S(2)}) collective-permute-start(bf16[2,9,2,128,256]{4,3,2,1,0:T(8,128)(2,1)} %slice.67), channel_id=1, source_target_pairs={{32,0},{64,32},{96,64},{0,96},{33,1},{65,33},{97,65},{1,97},{34,2}... | collective-permute-start | bytes 7077896 | tf_op jit(solution)/shard_map/ppermute | solution.py:37
  227.4 3.4 %slice.68 = bf16[2,9,2,128,256]{4,3,2,1,0:T(8,128)(2,1)} slice(bf16[4,9,2,128,256]{4,3,2,1,0:T(8,128)(2,1)} %collective-permute-done.6), slice={[2:4], [0:9], [0:2], [0:128], [0:256]} | slice | bytes 4718592 | tf_op jit(solution)/shard_map/slice | solution.py:45
  230.8 1.6 convolution_bitcast_fusion.3
  233.3 2.7 copy.103
  236.0 2.7 copy.99
  238.7 3.0 %convolution_bitcast_fusion = f32[9,2,64,512]{3,2,1,0:T(8,128)} fusion(bf16[9,2,512,256,1]{3,2,1,4,0:T(8,128)(2,1)S(1)} %bitcast.191, bf16[9,2,64,2,256]{4,2,0,3,1:T(8,128)(2,1)S(1)} %pad_maximum_fusion.18), kind=kOutput, calls=%fused_computation.24 | convolution fusion | flops 603979776 | bytes 8257536 | tf_op jit(solution)/shard_map/fqipw,fpjw->fqij/dot_general | solution.py:106
  241.7 3.0 %convolution_bitcast_fusion.2 = f32[9,2,64,512]{3,2,1,0:T(8,128)} fusion(bf16[9,2,512,256,1]{3,2,1,4,0:T(8,128)(2,1)S(1)} %bitcast.192, bf16[9,2,64,2,256]{4,2,0,3,1:T(8,128)(2,1)S(1)} %pad_maximum_fusion.18), kind=kOutput, calls=%fused_computation.26 | convolution fusion | flops 603979776 | bytes 8257536 | tf_op jit(solution)/shard_map/fqipw,fpjw->fqij/dot_general | solution.py:106
  244.8 3.0 collective-permute-done.13
  247.7 4.2 %collective-permute-done.15 = bf16[2,7,2,128,256]{4,3,2,1,0:T(8,128)(2,1)S(1)} collective-permute-done((bf16[2,7,2,128,256]{4,3,2,1,0:T(8,128)(2,1)}, bf16[2,7,2,128,256]{4,3,2,1,0:T(8,128)(2,1)S(1)}, u32[]{:S(2)}, u32[]{:S(2)}) %collective-permute-start.15) | collective-permute-done | bytes 1835040 | tf_op jit(solution)/shard_map/ppermute | solution.py:37
  252.4 20.0 %conditional.6 = (bf16[7,2,2048,256]{3,2,1,0:T(8,128)(2,1)}) conditional(s32[]{:T(128)} %clamp.9, (bf16[7,2,4,2,64,256]{5,4,3,2,1,0:T(8,128)(2,1)S(1)}, bf16[7,2,4,2,64,256]{5,4,3,2,1,0:T(8,128)(2,1)S(1)}, bf16[7,2,4,2,64,256]{5,4,3,2,1,0:T(8,128)(2,1)S(1)}, bf16[7,2,4,2,64,256]{5,4,3,2,1,0:T(8,128)(2,1)S(1)}) %tuple.119, ...), branch_computations={%region_9.10_spmd, %region_10.11_spmd, %region_11.12_spmd, %region... | conditional | flops 22020096 | bytes 58720264 | solution.py:58
  252.5 6.5 %pad_maximum_fusion.8 = bf16[7,2,4,2,4,64,256]{6,5,3,2,1,0,4:T(8,128)(2,1)} fusion(bf16[7,2,4,2,1,64,256]{6,5,3,2,1,0,4:T(8,128)(2,1)S(1)} %bitcast.174, bf16[7,2,4,2,1,64,256]{6,5,3,2,1,0,4:T(8,128)(2,1)S(1)} %bitcast.182, bf16[7,2,4,2,1,64,256]{6,5,3,2,1,0,4:T(8,128)(2,1)S(1)} %bitcast.166, bf16[7,2,4,2,1,64,256]{6,5,3,2,1,0,4:T(8,128)(2,1)S(1)} %bitcast.158), kind=kLoop, calls=%fused_computation.8 | loop fusion | flops 22020096 | bytes 29360128 | tf_op jit(solution)/shard_map/cond/branch_0_fun/stack | solution.py:54
  258.9 13.5 %copy.90 = bf16[7,2,4,2,4,64,256]{6,5,4,3,2,1,0:T(8,128)(2,1)} copy(bf16[7,2,4,2,4,64,256]{6,5,3,2,1,0,4:T(8,128)(2,1)} %pad_maximum_fusion.8) | data formatting | bytes 29360128 | tf_op jit(solution)/shard_map/cond/branch_0_fun/stack | solution.py:54
  272.4 13.2 %fusion.3 = f32[7,2,64,2048]{3,2,1,0:T(8,128)} fusion(bf16[7,2,2048,256]{3,2,1,0:T(8,128)(2,1)} %get-tuple-element.257, bf16[7,2,64,2,256]{4,2,0,3,1:T(8,128)(2,1)} %pad_maximum_fusion.19), kind=kOutput, calls=%fused_computation.22 | convolution fusion | flops 1879048192 | bytes 22937600 | tf_op jit(solution)/shard_map/fqipw,fpjw->fqij/dot_general | solution.py:111
  285.6 2.8 pad_maximum_fusion.16
  289.1 1.6 convolution_bitcast_fusion.1
  293.1 6.4 %conditional.7 = (f32[16,2,64,2048]{3,2,1,0:T(8,128)}) conditional(s32[]{:T(128)} %clamp.8, (f32[9,2,64,512]{3,2,1,0:T(8,128)S(1)}, f32[9,2,64,512]{3,2,1,0:T(8,128)S(1)}, f32[9,2,64,512]{3,2,1,0:T(8,128)S(1)}, f32[9,2,64,512]{3,2,1,0:T(8,128)S(1)}, f32[7,2,64,2048]{3,2,1,0:T(8,128)S(1)}) %tuple.127, ...), branch_computations={%region_13.14_spmd, %region_14.15_spmd, %region_15.16_spmd, %regio... | conditional | flops 16777216 | bytes 33554440 | solution.py:123
  293.1 6.4 %pad_maximum_fusion.12 = f32[16,2,64,2048]{3,2,1,0:T(8,128)} fusion(f32[7,2,64,2048]{3,2,1,0:T(8,128)S(1)} %get-tuple-element.214, f32[9,2,64,512]{3,2,1,0:T(8,128)S(1)} %get-tuple-element.213, f32[9,2,64,512]{3,2,1,0:T(8,128)S(1)} %get-tuple-element.212, f32[9,2,64,512]{3,2,1,0:T(8,128)S(1)} %get-tuple-element.211, f32[9,2,64,512]{3,2,1,0:T(8,128)S(1)} %get-tuple-element.210), kind=kLoop, calls=%fused_computation.12 | loop fusion | flops 16777216 | bytes 33554432 | tf_op jit(solution)/shard_map/cond/branch_0_fun/concatenate | solution.py:118
  (66 shorter events, 19.7 us)
Async XLA Ops:
  65.4 27.9 %collective-permute-start = (bf16[9,2,128,256]{3,2,1,0:T(8,128)(2,1)S(1)}, bf16[9,2,128,256]{3,2,1,0:T(8,128)(2,1)S(1)}, u32[]{:S(2)}, u32[]{:S(2)}) collective-permute-start(bf16[9,2,128,256]{3,2,1,0:T(8,128)(2,1)S(1)} %slice.49), channel_id=1, source_target_pairs={{4,0},{8,4},{12,8},{0,12},{5,1},{9,5},{13,9},{1,13},{6,2},{10,6},{... | collective-permute-start | bytes 3538952 | tf_op jit(solution)/shard_map/ppermute | solution.py:37
  68.3 28.9 %collective-permute-start.2 = (bf16[9,2,128,256]{3,2,1,0:T(8,128)(2,1)S(1)}, bf16[9,2,128,256]{3,2,1,0:T(8,128)(2,1)}, u32[]{:S(2)}, u32[]{:S(2)}) collective-permute-start(bf16[9,2,128,256]{3,2,1,0:T(8,128)(2,1)S(1)} %slice.49), channel_id=1, source_target_pairs={{12,0},{0,4},{4,8},{8,12},{13,1},{1,5},{5,9},{9,13},{14,2},{2,6},{... | collective-permute-start | bytes 3538952 | tf_op jit(solution)/shard_map/ppermute | solution.py:37
  76.0 23.2 %collective-permute-start.8 = (bf16[7,2,128,256]{3,2,1,0:T(8,128)(2,1)S(1)}, bf16[7,2,128,256]{3,2,1,0:T(8,128)(2,1)}, u32[]{:S(2)}, u32[]{:S(2)}) collective-permute-start(bf16[7,2,128,256]{3,2,1,0:T(8,128)(2,1)S(1)} %slice.57), channel_id=1, source_target_pairs={{32,0},{64,32},{96,64},{0,96},{33,1},{65,33},{97,65},{1,97},{34,2}... | collective-permute-start | bytes 2752520 | tf_op jit(solution)/shard_map/ppermute | solution.py:37
  80.1 24.8 %collective-permute-start.10 = (bf16[7,2,128,256]{3,2,1,0:T(8,128)(2,1)S(1)}, bf16[7,2,128,256]{3,2,1,0:T(8,128)(2,1)}, u32[]{:S(2)}, u32[]{:S(2)}) collective-permute-start(bf16[7,2,128,256]{3,2,1,0:T(8,128)(2,1)S(1)} %slice.57), channel_id=1, source_target_pairs={{96,0},{0,32},{32,64},{64,96},{97,1},{1,33},{33,65},{65,97},{98,2}... | collective-permute-start | bytes 2752520 | tf_op jit(solution)/shard_map/ppermute | solution.py:37
  93.3 5.3 %copy-start.2 = (bf16[9,2,128,256]{3,2,1,0:T(8,128)(2,1)}, bf16[9,2,128,256]{3,2,1,0:T(8,128)(2,1)S(1)}, u32[]{:S(2)}) copy-start(bf16[9,2,128,256]{3,2,1,0:T(8,128)(2,1)S(1)} %collective-permute-done) | copy-start | bytes 3538948
  93.3 15.4 %collective-permute-start.1 = (bf16[9,1,128,256]{3,2,1,0:T(8,128)(2,1)S(1)}, bf16[9,1,128,256]{3,2,1,0:T(8,128)(2,1)S(1)}, u32[]{:S(2)}, u32[]{:S(2)}) collective-permute-start(bf16[9,1,128,256]{3,2,1,0:T(8,128)(2,1)S(1)} %slice.65), channel_id=1, source_target_pairs={{4,0},{8,4},{12,8},{0,12},{5,1},{9,5},{13,9},{1,13},{6,2},{10,6},{... | collective-permute-start | bytes 1769480 | tf_op jit(solution)/shard_map/ppermute | solution.py:37
  98.2 15.1 %collective-permute-start.3 = (bf16[9,1,128,256]{3,2,1,0:T(8,128)(2,1)S(1)}, bf16[9,1,128,256]{3,2,1,0:T(8,128)(2,1)S(1)}, u32[]{:S(2)}, u32[]{:S(2)}) collective-permute-start(bf16[9,1,128,256]{3,2,1,0:T(8,128)(2,1)S(1)} %slice.66), channel_id=1, source_target_pairs={{12,0},{0,4},{4,8},{8,12},{13,1},{1,5},{5,9},{9,13},{14,2},{2,6},{... | collective-permute-start | bytes 1769480 | tf_op jit(solution)/shard_map/ppermute | solution.py:37
  98.6 14.8 %copy-start.3 = (bf16[9,2,128,256]{3,2,1,0:T(8,128)(2,1)S(1)}, bf16[9,2,128,256]{3,2,1,0:T(8,128)(2,1)}, u32[]{:S(2)}) copy-start(bf16[9,2,128,256]{3,2,1,0:T(8,128)(2,1)} %copy-done.2) | copy-start | bytes 3538948
  101.1 22.1 %collective-permute-start.9 = (bf16[7,1,128,256]{3,2,1,0:T(8,128)(2,1)}, bf16[7,1,128,256]{3,2,1,0:T(8,128)(2,1)}, u32[]{:S(2)}, u32[]{:S(2)}) collective-permute-start(bf16[7,1,128,256]{3,2,1,0:T(8,128)(2,1)} %slice.70), channel_id=1, source_target_pairs={{32,0},{64,32},{96,64},{0,96},{33,1},{65,33},{97,65},{1,97},{34,2}... | collective-permute-start | bytes 1376264 | tf_op jit(solution)/shard_map/ppermute | solution.py:37
  106.7 17.5 %collective-permute-start.11 = (bf16[7,1,128,256]{3,2,1,0:T(8,128)(2,1)}, bf16[7,1,128,256]{3,2,1,0:T(8,128)(2,1)}, u32[]{:S(2)}, u32[]{:S(2)}) collective-permute-start(bf16[7,1,128,256]{3,2,1,0:T(8,128)(2,1)} %slice.71), channel_id=1, source_target_pairs={{96,0},{0,32},{32,64},{64,96},{97,1},{1,33},{33,65},{65,97},{98,2}... | collective-permute-start | bytes 1376264 | tf_op jit(solution)/shard_map/ppermute | solution.py:37
  117.0 110.4 %collective-permute-start.6 = (bf16[4,9,2,128,256]{4,3,2,1,0:T(8,128)(2,1)}, bf16[4,9,2,128,256]{4,3,2,1,0:T(8,128)(2,1)}, u32[]{:S(2)}, u32[]{:S(2)}) collective-permute-start(bf16[4,9,2,128,256]{4,3,2,1,0:T(8,128)(2,1)} %get-tuple-element.255), channel_id=1, source_target_pairs={{96,0},{0,32},{32,64},{64,96},{97,1},{1,33},{33,65},{65,97},{98,2}... | collective-permute-start | bytes 14155784 | tf_op jit(solution)/shard_map/ppermute | solution.py:37
  118.8 101.5 %collective-permute-start.4 = (bf16[4,9,2,128,256]{4,3,2,1,0:T(8,128)(2,1)}, bf16[4,9,2,128,256]{4,3,2,1,0:T(8,128)(2,1)}, u32[]{:S(2)}, u32[]{:S(2)}) collective-permute-start(bf16[4,9,2,128,256]{4,3,2,1,0:T(8,128)(2,1)} %get-tuple-element.255), channel_id=1, source_target_pairs={{32,0},{64,32},{96,64},{0,96},{33,1},{65,33},{97,65},{1,97},{34,2}... | collective-permute-start | bytes 14155784 | tf_op jit(solution)/shard_map/ppermute | solution.py:37
  128.6 83.7 %copy-start.4 = (bf16[4,7,2,128,256]{4,3,2,1,0:T(8,128)(2,1)S(1)}, bf16[4,7,2,128,256]{4,3,2,1,0:T(8,128)(2,1)}, u32[]{:S(2)}) copy-start(bf16[4,7,2,128,256]{4,3,2,1,0:T(8,128)(2,1)} %get-tuple-element.256) | copy-start | bytes 11010052
  128.6 78.9 %collective-permute-start.12 = (bf16[4,7,2,128,256]{4,3,2,1,0:T(8,128)(2,1)}, bf16[4,7,2,128,256]{4,3,2,1,0:T(8,128)(2,1)S(1)}, u32[]{:S(2)}, u32[]{:S(2)}) collective-permute-start(bf16[4,7,2,128,256]{4,3,2,1,0:T(8,128)(2,1)} %get-tuple-element.256), channel_id=1, source_target_pairs={{4,0},{8,4},{12,8},{0,12},{5,1},{9,5},{13,9},{1,13},{6,2},{10,6},{... | collective-permute-start | bytes 11010056 | tf_op jit(solution)/shard_map/ppermute | solution.py:37
  128.7 81.8 %collective-permute-start.14 = (bf16[4,7,2,128,256]{4,3,2,1,0:T(8,128)(2,1)}, bf16[4,7,2,128,256]{4,3,2,1,0:T(8,128)(2,1)S(1)}, u32[]{:S(2)}, u32[]{:S(2)}) collective-permute-start(bf16[4,7,2,128,256]{4,3,2,1,0:T(8,128)(2,1)} %get-tuple-element.256), channel_id=1, source_target_pairs={{12,0},{0,4},{4,8},{8,12},{13,1},{1,5},{5,9},{9,13},{14,2},{2,6},{... | collective-permute-start | bytes 11010056 | tf_op jit(solution)/shard_map/ppermute | solution.py:37
  208.9 38.8 %collective-permute-start.13 = (bf16[2,7,2,128,256]{4,3,2,1,0:T(8,128)(2,1)}, bf16[2,7,2,128,256]{4,3,2,1,0:T(8,128)(2,1)S(1)}, u32[]{:S(2)}, u32[]{:S(2)}) collective-permute-start(bf16[2,7,2,128,256]{4,3,2,1,0:T(8,128)(2,1)} %slice.72), channel_id=1, source_target_pairs={{4,0},{8,4},{12,8},{0,12},{5,1},{9,5},{13,9},{1,13},{6,2},{10,6},{... | collective-permute-start | bytes 5505032 | tf_op jit(solution)/shard_map/ppermute | solution.py:37
  211.9 40.0 %collective-permute-start.15 = (bf16[2,7,2,128,256]{4,3,2,1,0:T(8,128)(2,1)}, bf16[2,7,2,128,256]{4,3,2,1,0:T(8,128)(2,1)S(1)}, u32[]{:S(2)}, u32[]{:S(2)}) collective-permute-start(bf16[2,7,2,128,256]{4,3,2,1,0:T(8,128)(2,1)} %slice.73), channel_id=1, source_target_pairs={{12,0},{0,4},{4,8},{8,12},{13,1},{1,5},{5,9},{9,13},{14,2},{2,6},{... | collective-permute-start | bytes 5505032 | tf_op jit(solution)/shard_map/ppermute | solution.py:37
  223.7 61.9 %collective-permute-start.5 = (bf16[2,9,2,128,256]{4,3,2,1,0:T(8,128)(2,1)}, bf16[2,9,2,128,256]{4,3,2,1,0:T(8,128)(2,1)}, u32[]{:S(2)}, u32[]{:S(2)}) collective-permute-start(bf16[2,9,2,128,256]{4,3,2,1,0:T(8,128)(2,1)} %slice.67), channel_id=1, source_target_pairs={{32,0},{64,32},{96,64},{0,96},{33,1},{65,33},{97,65},{1,97},{34,2}... | collective-permute-start | bytes 7077896 | tf_op jit(solution)/shard_map/ppermute | solution.py:37
  230.8 54.8 %collective-permute-start.7 = (bf16[2,9,2,128,256]{4,3,2,1,0:T(8,128)(2,1)}, bf16[2,9,2,128,256]{4,3,2,1,0:T(8,128)(2,1)}, u32[]{:S(2)}, u32[]{:S(2)}) collective-permute-start(bf16[2,9,2,128,256]{4,3,2,1,0:T(8,128)(2,1)} %slice.68), channel_id=1, source_target_pairs={{96,0},{0,32},{32,64},{64,96},{97,1},{1,33},{33,65},{65,97},{98,2}... | collective-permute-start | bytes 7077896 | tf_op jit(solution)/shard_map/ppermute | solution.py:37
  288.4 2.4 slice-start
  289.1 2.6 slice-start.1
  289.1 3.3 %copy-start = (f32[9,2,64,512]{3,2,1,0:T(8,128)S(1)}, f32[9,2,64,512]{3,2,1,0:T(8,128)}, u32[]{:S(2)}) copy-start(f32[9,2,64,512]{3,2,1,0:T(8,128)} %convolution_bitcast_fusion) | copy-start | bytes 7077892
  289.1 3.9 %copy-start.1 = (f32[9,2,64,512]{3,2,1,0:T(8,128)S(1)}, f32[9,2,64,512]{3,2,1,0:T(8,128)}, u32[]{:S(2)}) copy-start(f32[9,2,64,512]{3,2,1,0:T(8,128)} %convolution_bitcast_fusion.2) | copy-start | bytes 7077892

commit v2 on v1

--- a/solution.py
+++ b/solution.py
@@ -107,7 +107,8 @@
 
     by_z = [products(rows_low, p, (1, 2, 3, 0, 4, 5)) for p in ring_gather(first, "z", 0)]
     second = [jnp.transpose(p.reshape(shape), (1, 2, 0, 3, 4, 5)) for p in ring_gather(second, "x", 0)]
-    second = ordered_by_position(second, "x", 4).reshape(-1, 2, width * zs, groups * win_local)
+    second = [p.reshape(p.shape[0], 2, zs * pairs, channels, groups * win_local) for p in second]
+    second = ordered_by_position(second, "x", 3).reshape(-1, 2, width * zs, groups * win_local)
     high = jnp.einsum(
         "fqipw,fpjw->fqij", rows_high, second, preferred_element_type=jnp.float32
     )

time: 300 us -> 297 us (0.990)
  local copies, waits for them, and re-layouts: 66.4 us -> 52.8 us
  waiting for transfers between devices: 108 us -> 118 us
    another operation x1 -> x0, local copies, waits for them, and re-layouts: 13.5 us -> none  [arrangement(): jnp.stack([blocks[(k - at) % size] for k in range(size)], axis=stack_axis)]
    ppermute x16, waiting for transfers between devices: 108 us -> 118 us  [shifted(): lax.ppermute(block, axis, [((i + distance) % size, i) for i in range(size)])]
  transfers between devices with their start and end apart: 16 -> 16, of which waited for: 8 -> 10; matrix products, arithmetic and copies ran while one was open for 28% -> 24% of each run, Pallas kernels for 0% -> 0%
where the time goes in v2:
time: 297 us; the launch traced here: 296 us
  waiting for transfers between devices  118 us (40%)
  local copies, waits for them, and re-layouts  52.8 us (18%)
  other arithmetic  37.6 us (13%)
  blocking collectives  31.3 us (11%)
  matrix products  28.8 us (10%)
  starting transfers between devices  26.4 us (9%)
    ppermute x16, waiting for transfers between devices, shifted(): lax.ppermute(block, axis, [((i + distance) % size, i) for i in range(size)])  118 us
    all_to_all x1, blocking collectives, per_device(): lax.all_to_all(outgoing, ('ylo', 'yhi', 'core'), 0, 0, tiled=True)  31.3 us
    ppermute x16, starting transfers between devices, shifted(): lax.ppermute(block, axis, [((i + distance) % size, i) for i in range(size)])  26.4 us
    slice x6, local copies, waits for them, and re-layouts, per_device(): low, high = (panel[:split], panel[split:])  17.7 us
    another operation x3, other arithmetic, arrangement(): jnp.stack([blocks[(k - at) % size] for k in range(size)], axis=stack_axis)  13.2 us
    dot_general x1, matrix products, per_device(): jnp.einsum('fqipw,fpjw->fqij', rows_high, second, preferred_element_type=...  13.2 us
    dot_general x4, matrix products, products(): jnp.einsum('fqipw,fpjw->fqij', part, block, preferred_element_type=jnp.fl...  9.37 us
    slice x4, local copies, waits for them, and re-layouts, ring_gather(): lax.slice_in_dim(behind, half, 2 * half, axis=split_axis)  7.73 us
  transfers between devices with their start and end apart: 16, of which 10 were waited for; matrix products, arithmetic and copies ran while one was open for 24% of the time, Pallas kernels for 0%

profile of v2, /device:TPU:0, one launch (start us, length us, event | category | flops | bytes accessed | tf_op | source)
XLA Modules:
  0.0 295.7 jit_solution(16705783629229842736)
XLA Ops:
  2.3 1.9 multiply_convert_fusion.1
  4.7 7.5 %maximum_minimum_fusion = bf16[64,64,1024]{2,1,0:T(8,128)(2,1)} fusion(bf16[64,64,1024]{2,1,0:T(8,128)(2,1)} %param.21, bf16[64]{0:T(256)(128)(2,1)S(1)} %multiply_convert_fusion.2, bf16[64]{0:T(256)(128)(2,1)S(1)} %fusion.18), kind=kLoop, calls=%fused_computation.18 | loop fusion | flops 8388608 | bytes 16777472 | tf_op jit(solution)/shard_map/min | solution.py:66
  12.2 6.3 %fusion.2 = bf16[128,4096]{1,0:T(8,128)(2,1)S(1)} fusion(bf16[1024,128]{0,1:T(8,128)(2,1)S(1)} %convert_element_type.55, bf16[4096,1024]{1,0:T(8,128)(2,1)} %bitcast.230, f32[4096]{0:T(1024)S(1)} %select_n.40), kind=kOutput, calls=%fused_computation.20 | convolution fusion | flops 1074790400 | bytes 9715712 | tf_op jit(solution)/shard_map/dot_general | solution.py:69
  18.7 31.3 %all_to_all.5 = bf16[8,32,4096]{2,1,0:T(8,128)(2,1)S(1)} all-to-all(bf16[8,32,4096]{2,1,0:T(8,128)(2,1)S(1)} %bitcast.251), channel_id=1, replica_groups=mesh['z'=4,'ylo'=2,'x'=4,'yhi'=2,'core'=2] {'ylo','yhi','core'}, dimensions={0} | all-to-all | bytes 4194304 | tf_op jit(solution)/shard_map/all_to_all | solution.py:85
  50.0 5.5 %reshape.287 = bf16[2,4,16,2,64,64]{5,4,3,2,1,0:T(8,128)(2,1)} reshape(bf16[8,32,4096]{2,1,0:T(8,128)(2,1)S(1)} %all_to_all.5) | data formatting | bytes 4194304 | tf_op jit(solution)/shard_map/reshape | solution.py:86
  55.5 2.5 slice.64
  58.0 3.7 %copy.155 = bf16[9,2,2,64,4,64]{5,4,3,2,1,0:T(4,128)(2,1)} copy(bf16[9,2,2,64,4,64]{5,3,1,0,4,2:T(8,128)(2,1)S(1)} %slice.64) | data formatting | bytes 2359296 | tf_op jit(solution)/shard_map/slice | solution.py:93
  61.7 3.7 %slice.49 = bf16[9,2,128,256]{3,2,1,0:T(8,128)(2,1)S(1)} reshape(bf16[9,2,2,64,4,64]{5,4,3,2,1,0:T(4,128)(2,1)} %copy.155) | data formatting | bytes 2359296 | tf_op jit(solution)/shard_map/slice | solution.py:93
  65.4 2.8 collective-permute-start
  68.3 1.7 slice.69
  69.9 2.9 copy.165
  72.9 3.2 %slice.57 = bf16[7,2,128,256]{3,2,1,0:T(8,128)(2,1)S(1)} reshape(bf16[7,2,2,64,4,64]{5,4,3,2,1,0:T(4,128)(2,1)} %copy.165) | data formatting | bytes 1835008 | tf_op jit(solution)/shard_map/slice | solution.py:93
  76.0 4.1 %collective-permute-start.8 = (bf16[7,2,128,256]{3,2,1,0:T(8,128)(2,1)S(1)}, bf16[7,2,128,256]{3,2,1,0:T(8,128)(2,1)}, u32[]{:S(2)}, u32[]{:S(2)}) collective-permute-start(bf16[7,2,128,256]{3,2,1,0:T(8,128)(2,1)S(1)} %slice.57), channel_id=1, source_target_pairs={{32,0},{64,32},{96,64},{0,96},{33,1},{65,33},{97,65},{1,97},{34,2}... | collective-permute-start | bytes 2752520 | tf_op jit(solution)/shard_map/ppermute | solution.py:37
  81.0 12.3 %collective-permute-done = bf16[9,2,128,256]{3,2,1,0:T(8,128)(2,1)S(1)} collective-permute-done((bf16[9,2,128,256]{3,2,1,0:T(8,128)(2,1)S(1)}, bf16[9,2,128,256]{3,2,1,0:T(8,128)(2,1)S(1)}, u32[]{:S(2)}, u32[]{:S(2)}) %collective-permute-start) | collective-permute-done | bytes 1179680 | tf_op jit(solution)/shard_map/ppermute | solution.py:37
  93.3 3.8 %collective-permute-start.1 = (bf16[9,1,128,256]{3,2,1,0:T(8,128)(2,1)S(1)}, bf16[9,1,128,256]{3,2,1,0:T(8,128)(2,1)S(1)}, u32[]{:S(2)}, u32[]{:S(2)}) collective-permute-start(bf16[9,1,128,256]{3,2,1,0:T(8,128)(2,1)S(1)} %slice.65), channel_id=1, source_target_pairs={{4,0},{8,4},{12,8},{0,12},{5,1},{9,5},{13,9},{1,13},{6,2},{10,6},{... | collective-permute-start | bytes 1769480 | tf_op jit(solution)/shard_map/ppermute | solution.py:37
  99.3 1.8 slice.70
  101.1 3.8 %collective-permute-start.9 = (bf16[7,1,128,256]{3,2,1,0:T(8,128)(2,1)}, bf16[7,1,128,256]{3,2,1,0:T(8,128)(2,1)}, u32[]{:S(2)}, u32[]{:S(2)}) collective-permute-start(bf16[7,1,128,256]{3,2,1,0:T(8,128)(2,1)} %slice.70), channel_id=1, source_target_pairs={{32,0},{64,32},{96,64},{0,96},{33,1},{65,33},{97,65},{1,97},{34,2}... | collective-permute-start | bytes 1376264 | tf_op jit(solution)/shard_map/ppermute | solution.py:37
  104.9 1.8 slice.71
  106.7 2.0 collective-permute-done.1
  108.7 4.6 %collective-permute-done.3 = bf16[9,1,128,256]{3,2,1,0:T(8,128)(2,1)S(1)} collective-permute-done((bf16[9,1,128,256]{3,2,1,0:T(8,128)(2,1)S(1)}, bf16[9,1,128,256]{3,2,1,0:T(8,128)(2,1)S(1)}, u32[]{:S(2)}, u32[]{:S(2)}) %collective-permute-start.3) | collective-permute-done | bytes 589856 | tf_op jit(solution)/shard_map/ppermute | solution.py:37
  113.4 3.6 %conditional.4 = (bf16[4,9,2,128,256]{4,3,2,1,0:T(8,128)(2,1)}) conditional(s32[]{:T(128)} %clamp.9, (bf16[9,2,128,256]{3,2,1,0:T(8,128)(2,1)S(1)}, bf16[9,2,128,256]{3,2,1,0:T(8,128)(2,1)S(1)}, bf16[9,2,128,256]{3,2,1,0:T(8,128)(2,1)S(1)}, bf16[9,2,128,256]{3,2,1,0:T(8,128)(2,1)}) %tuple.131, ...), branch_computations={%region_1.2_spmd, %region_2.3_spmd, %region_3.4_spmd, %region_4.5_... | conditional | flops 7077888 | bytes 9437192 | solution.py:58
  113.4 3.6 %pad_maximum_fusion = bf16[4,9,2,128,256]{4,3,2,1,0:T(8,128)(2,1)} fusion(bf16[1,9,2,128,256]{4,3,2,1,0:T(8,128)(2,1)} %bitcast.3, bf16[1,9,2,128,256]{4,3,2,1,0:T(8,128)(2,1)S(1)} %bitcast.239, bf16[1,9,2,128,256]{4,3,2,1,0:T(8,128)(2,1)S(1)} %bitcast.235, bf16[1,9,2,128,256]{4,3,2,1,0:T(8,128)(2,1)S(1)} %bitcast.226), kind=kLoop, calls=%fused_computation | loop fusion | flops 7077888 | bytes 9437184 | tf_op jit(solution)/shard_map/cond/branch_0_fun/stack | solution.py:54
  117.0 1.8 collective-permute-start.6
  118.8 2.2 collective-permute-start.4
  125.2 3.4 %conditional.5 = (bf16[4,7,2,128,256]{4,3,2,1,0:T(8,128)(2,1)}) conditional(s32[]{:T(128)} %clamp.8, (bf16[7,2,128,256]{3,2,1,0:T(8,128)(2,1)S(1)}, bf16[7,2,128,256]{3,2,1,0:T(8,128)(2,1)}, bf16[7,2,128,256]{3,2,1,0:T(8,128)(2,1)S(1)}, bf16[7,2,128,256]{3,2,1,0:T(8,128)(2,1)}) %tuple.64, ...), branch_computations={%region_5.6_spmd, %region_6.7_spmd, %region_7.8_spmd, %region_8.9_... | conditional | flops 5505024 | bytes 7340040 | solution.py:58
  125.3 3.3 %pad_maximum_fusion.4 = bf16[4,7,2,128,256]{4,3,2,1,0:T(8,128)(2,1)} fusion(bf16[1,7,2,128,256]{4,3,2,1,0:T(8,128)(2,1)} %bitcast.19, bf16[1,7,2,128,256]{4,3,2,1,0:T(8,128)(2,1)S(1)} %bitcast.245, bf16[1,7,2,128,256]{4,3,2,1,0:T(8,128)(2,1)} %bitcast.17, bf16[1,7,2,128,256]{4,3,2,1,0:T(8,128)(2,1)S(1)} %bitcast.231), kind=kLoop, calls=%fused_computation.4 | loop fusion | flops 5505024 | bytes 7340032 | tf_op jit(solution)/shard_map/cond/branch_0_fun/stack | solution.py:54
  128.6 2.0 collective-permute-start.14
  130.6 76.9 %collective-permute-done.12 = bf16[4,7,2,128,256]{4,3,2,1,0:T(8,128)(2,1)S(1)} collective-permute-done((bf16[4,7,2,128,256]{4,3,2,1,0:T(8,128)(2,1)}, bf16[4,7,2,128,256]{4,3,2,1,0:T(8,128)(2,1)S(1)}, u32[]{:S(2)}, u32[]{:S(2)}) %collective-permute-start.12) | collective-permute-done | bytes 3670048 | tf_op jit(solution)/shard_map/ppermute | solution.py:37
  212.6 2.7 copy.157
  215.3 5.0 %collective-permute-done.4 = bf16[4,9,2,128,256]{4,3,2,1,0:T(8,128)(2,1)} collective-permute-done((bf16[4,9,2,128,256]{4,3,2,1,0:T(8,128)(2,1)}, bf16[4,9,2,128,256]{4,3,2,1,0:T(8,128)(2,1)}, u32[]{:S(2)}, u32[]{:S(2)}) %collective-permute-start.4) | collective-permute-done | bytes 4718624 | tf_op jit(solution)/shard_map/ppermute | solution.py:37
  220.3 3.3 %slice.67 = bf16[2,9,2,128,256]{4,3,2,1,0:T(8,128)(2,1)} slice(bf16[4,9,2,128,256]{4,3,2,1,0:T(8,128)(2,1)} %collective-permute-done.4), slice={[0:2], [0:9], [0:2], [0:128], [0:256]} | slice | bytes 4718592 | tf_op jit(solution)/shard_map/slice | solution.py:44
  223.6 3.7 %collective-permute-start.5 = (bf16[2,9,2,128,256]{4,3,2,1,0:T(8,128)(2,1)}, bf16[2,9,2,128,256]{4,3,2,1,0:T(8,128)(2,1)}, u32[]{:S(2)}, u32[]{:S(2)}) collective-permute-start(bf16[2,9,2,128,256]{4,3,2,1,0:T(8,128)(2,1)} %slice.67), channel_id=1, source_target_pairs={{32,0},{64,32},{96,64},{0,96},{33,1},{65,33},{97,65},{1,97},{34,2}... | collective-permute-start | bytes 7077896 | tf_op jit(solution)/shard_map/ppermute | solution.py:37
  227.3 3.4 %slice.68 = bf16[2,9,2,128,256]{4,3,2,1,0:T(8,128)(2,1)} slice(bf16[4,9,2,128,256]{4,3,2,1,0:T(8,128)(2,1)} %collective-permute-done.6), slice={[2:4], [0:9], [0:2], [0:128], [0:256]} | slice | bytes 4718592 | tf_op jit(solution)/shard_map/slice | solution.py:45
  233.1 2.7 copy.163
  235.9 2.7 copy.159
  238.6 3.1 %convolution_bitcast_fusion = f32[9,2,64,512]{3,2,1,0:T(8,128)} fusion(bf16[9,2,512,256,1]{3,2,1,4,0:T(8,128)(2,1)S(1)} %bitcast.223, bf16[9,2,64,2,256]{4,2,0,3,1:T(8,128)(2,1)S(1)} %pad_maximum_fusion.18), kind=kOutput, calls=%fused_computation.24 | convolution fusion | flops 603979776 | bytes 8257536 | tf_op jit(solution)/shard_map/fqipw,fpjw->fqij/dot_general | solution.py:106
  241.7 3.0 %convolution_bitcast_fusion.2 = f32[9,2,64,512]{3,2,1,0:T(8,128)} fusion(bf16[9,2,512,256,1]{3,2,1,4,0:T(8,128)(2,1)S(1)} %bitcast.224, bf16[9,2,64,2,256]{4,2,0,3,1:T(8,128)(2,1)S(1)} %pad_maximum_fusion.18), kind=kOutput, calls=%fused_computation.26 | convolution fusion | flops 603979776 | bytes 8257536 | tf_op jit(solution)/shard_map/fqipw,fpjw->fqij/dot_general | solution.py:106
  244.7 3.0 %collective-permute-done.13 = bf16[2,7,2,128,256]{4,3,2,1,0:T(8,128)(2,1)S(1)} collective-permute-done((bf16[2,7,2,128,256]{4,3,2,1,0:T(8,128)(2,1)}, bf16[2,7,2,128,256]{4,3,2,1,0:T(8,128)(2,1)S(1)}, u32[]{:S(2)}, u32[]{:S(2)}) %collective-permute-start.13) | collective-permute-done | bytes 1835040 | tf_op jit(solution)/shard_map/ppermute | solution.py:37
  247.7 4.2 %collective-permute-done.15 = bf16[2,7,2,128,256]{4,3,2,1,0:T(8,128)(2,1)S(1)} collective-permute-done((bf16[2,7,2,128,256]{4,3,2,1,0:T(8,128)(2,1)}, bf16[2,7,2,128,256]{4,3,2,1,0:T(8,128)(2,1)S(1)}, u32[]{:S(2)}, u32[]{:S(2)}) %collective-permute-start.15) | collective-permute-done | bytes 1835040 | tf_op jit(solution)/shard_map/ppermute | solution.py:37
  252.4 6.3 %conditional.6 = (bf16[7,2,2048,256]{3,2,1,0:T(8,128)(2,1)}) conditional(s32[]{:T(128)} %clamp.9, (bf16[7,2,4,2,64,256]{5,4,3,2,1,0:T(8,128)(2,1)S(1)}, bf16[7,2,4,2,64,256]{5,4,3,2,1,0:T(8,128)(2,1)S(1)}, bf16[7,2,4,2,64,256]{5,4,3,2,1,0:T(8,128)(2,1)S(1)}, bf16[7,2,4,2,64,256]{5,4,3,2,1,0:T(8,128)(2,1)S(1)}) %tuple.119, ...), branch_computations={%region_9.10_spmd, %region_10.11_spmd, %region_11.12_spmd, %region... | conditional | flops 22020096 | bytes 29360136 | solution.py:58
  252.4 6.3 %pad_maximum_fusion.8 = bf16[7,2,8,4,64,256]{5,4,3,2,1,0:T(8,128)(2,1)} fusion(bf16[7,2,8,1,64,256]{5,4,3,2,1,0:T(8,128)(2,1)S(1)} %bitcast.206, bf16[7,2,8,1,64,256]{5,4,3,2,1,0:T(8,128)(2,1)S(1)} %bitcast.214, bf16[7,2,8,1,64,256]{5,4,3,2,1,0:T(8,128)(2,1)S(1)} %bitcast.198, bf16[7,2,8,1,64,256]{5,4,3,2,1,0:T(8,128)(2,1)S(1)} %bitcast.190), kind=kLoop, calls=%fused_computation.8 | loop fusion | flops 22020096 | bytes 29360128 | tf_op jit(solution)/shard_map/cond/branch_0_fun/stack | solution.py:54
  258.8 13.2 %fusion.3 = f32[7,2,64,2048]{3,2,1,0:T(8,128)} fusion(bf16[7,2,2048,256]{3,2,1,0:T(8,128)(2,1)} %get-tuple-element.257, bf16[7,2,64,2,256]{4,2,0,3,1:T(8,128)(2,1)} %pad_maximum_fusion.19), kind=kOutput, calls=%fused_computation.22 | convolution fusion | flops 1879048192 | bytes 22937600 | tf_op jit(solution)/shard_map/fqipw,fpjw->fqij/dot_general | solution.py:112
  271.9 3.2 %collective-permute-done.5 = bf16[2,9,2,128,256]{4,3,2,1,0:T(8,128)(2,1)} collective-permute-done((bf16[2,9,2,128,256]{4,3,2,1,0:T(8,128)(2,1)}, bf16[2,9,2,128,256]{4,3,2,1,0:T(8,128)(2,1)}, u32[]{:S(2)}, u32[]{:S(2)}) %collective-permute-start.5) | collective-permute-done | bytes 2359328 | tf_op jit(solution)/shard_map/ppermute | solution.py:37
  275.1 6.8 %collective-permute-done.7 = bf16[2,9,2,128,256]{4,3,2,1,0:T(8,128)(2,1)} collective-permute-done((bf16[2,9,2,128,256]{4,3,2,1,0:T(8,128)(2,1)}, bf16[2,9,2,128,256]{4,3,2,1,0:T(8,128)(2,1)}, u32[]{:S(2)}, u32[]{:S(2)}) %collective-permute-start.7) | collective-permute-done | bytes 2359328 | tf_op jit(solution)/shard_map/ppermute | solution.py:37
  281.9 2.8 pad_maximum_fusion.16
  285.4 1.6 convolution_bitcast_fusion.1
  289.4 6.4 %conditional.7 = (f32[16,2,64,2048]{3,2,1,0:T(8,128)}) conditional(s32[]{:T(128)} %clamp.8, (f32[9,2,64,512]{3,2,1,0:T(8,128)S(1)}, f32[9,2,64,512]{3,2,1,0:T(8,128)S(1)}, f32[9,2,64,512]{3,2,1,0:T(8,128)S(1)}, f32[9,2,64,512]{3,2,1,0:T(8,128)S(1)}, f32[7,2,64,2048]{3,2,1,0:T(8,128)S(1)}) %tuple.127, ...), branch_computations={%region_13.14_spmd, %region_14.15_spmd, %region_15.16_spmd, %regio... | conditional | flops 16777216 | bytes 33554440 | solution.py:124
  289.4 6.4 %pad_maximum_fusion.12 = f32[16,2,64,2048]{3,2,1,0:T(8,128)} fusion(f32[7,2,64,2048]{3,2,1,0:T(8,128)S(1)} %get-tuple-element.214, f32[9,2,64,512]{3,2,1,0:T(8,128)S(1)} %get-tuple-element.213, f32[9,2,64,512]{3,2,1,0:T(8,128)S(1)} %get-tuple-element.212, f32[9,2,64,512]{3,2,1,0:T(8,128)S(1)} %get-tuple-element.211, f32[9,2,64,512]{3,2,1,0:T(8,128)S(1)} %get-tuple-element.210), kind=kLoop, calls=%fused_computation.12 | loop fusion | flops 16777216 | bytes 33554432 | tf_op jit(solution)/shard_map/cond/branch_0_fun/concatenate | solution.py:119
  (65 shorter events, 21.3 us)
Async XLA Ops:
  65.4 27.9 %collective-permute-start = (bf16[9,2,128,256]{3,2,1,0:T(8,128)(2,1)S(1)}, bf16[9,2,128,256]{3,2,1,0:T(8,128)(2,1)S(1)}, u32[]{:S(2)}, u32[]{:S(2)}) collective-permute-start(bf16[9,2,128,256]{3,2,1,0:T(8,128)(2,1)S(1)} %slice.49), channel_id=1, source_target_pairs={{4,0},{8,4},{12,8},{0,12},{5,1},{9,5},{13,9},{1,13},{6,2},{10,6},{... | collective-permute-start | bytes 3538952 | tf_op jit(solution)/shard_map/ppermute | solution.py:37
  68.3 28.9 %collective-permute-start.2 = (bf16[9,2,128,256]{3,2,1,0:T(8,128)(2,1)S(1)}, bf16[9,2,128,256]{3,2,1,0:T(8,128)(2,1)}, u32[]{:S(2)}, u32[]{:S(2)}) collective-permute-start(bf16[9,2,128,256]{3,2,1,0:T(8,128)(2,1)S(1)} %slice.49), channel_id=1, source_target_pairs={{12,0},{0,4},{4,8},{8,12},{13,1},{1,5},{5,9},{9,13},{14,2},{2,6},{... | collective-permute-start | bytes 3538952 | tf_op jit(solution)/shard_map/ppermute | solution.py:37
  76.0 23.2 %collective-permute-start.8 = (bf16[7,2,128,256]{3,2,1,0:T(8,128)(2,1)S(1)}, bf16[7,2,128,256]{3,2,1,0:T(8,128)(2,1)}, u32[]{:S(2)}, u32[]{:S(2)}) collective-permute-start(bf16[7,2,128,256]{3,2,1,0:T(8,128)(2,1)S(1)} %slice.57), channel_id=1, source_target_pairs={{32,0},{64,32},{96,64},{0,96},{33,1},{65,33},{97,65},{1,97},{34,2}... | collective-permute-start | bytes 2752520 | tf_op jit(solution)/shard_map/ppermute | solution.py:37
  80.1 24.8 %collective-permute-start.10 = (bf16[7,2,128,256]{3,2,1,0:T(8,128)(2,1)S(1)}, bf16[7,2,128,256]{3,2,1,0:T(8,128)(2,1)}, u32[]{:S(2)}, u32[]{:S(2)}) collective-permute-start(bf16[7,2,128,256]{3,2,1,0:T(8,128)(2,1)S(1)} %slice.57), channel_id=1, source_target_pairs={{96,0},{0,32},{32,64},{64,96},{97,1},{1,33},{33,65},{65,97},{98,2}... | collective-permute-start | bytes 2752520 | tf_op jit(solution)/shard_map/ppermute | solution.py:37
  93.3 5.3 %copy-start.2 = (bf16[9,2,128,256]{3,2,1,0:T(8,128)(2,1)}, bf16[9,2,128,256]{3,2,1,0:T(8,128)(2,1)S(1)}, u32[]{:S(2)}) copy-start(bf16[9,2,128,256]{3,2,1,0:T(8,128)(2,1)S(1)} %collective-permute-done) | copy-start | bytes 3538948
  93.3 15.4 %collective-permute-start.1 = (bf16[9,1,128,256]{3,2,1,0:T(8,128)(2,1)S(1)}, bf16[9,1,128,256]{3,2,1,0:T(8,128)(2,1)S(1)}, u32[]{:S(2)}, u32[]{:S(2)}) collective-permute-start(bf16[9,1,128,256]{3,2,1,0:T(8,128)(2,1)S(1)} %slice.65), channel_id=1, source_target_pairs={{4,0},{8,4},{12,8},{0,12},{5,1},{9,5},{13,9},{1,13},{6,2},{10,6},{... | collective-permute-start | bytes 1769480 | tf_op jit(solution)/shard_map/ppermute | solution.py:37
  98.2 15.1 %collective-permute-start.3 = (bf16[9,1,128,256]{3,2,1,0:T(8,128)(2,1)S(1)}, bf16[9,1,128,256]{3,2,1,0:T(8,128)(2,1)S(1)}, u32[]{:S(2)}, u32[]{:S(2)}) collective-permute-start(bf16[9,1,128,256]{3,2,1,0:T(8,128)(2,1)S(1)} %slice.66), channel_id=1, source_target_pairs={{12,0},{0,4},{4,8},{8,12},{13,1},{1,5},{5,9},{9,13},{14,2},{2,6},{... | collective-permute-start | bytes 1769480 | tf_op jit(solution)/shard_map/ppermute | solution.py:37
  98.6 14.8 %copy-start.3 = (bf16[9,2,128,256]{3,2,1,0:T(8,128)(2,1)S(1)}, bf16[9,2,128,256]{3,2,1,0:T(8,128)(2,1)}, u32[]{:S(2)}) copy-start(bf16[9,2,128,256]{3,2,1,0:T(8,128)(2,1)} %copy-done.2) | copy-start | bytes 3538948
  101.1 22.0 %collective-permute-start.9 = (bf16[7,1,128,256]{3,2,1,0:T(8,128)(2,1)}, bf16[7,1,128,256]{3,2,1,0:T(8,128)(2,1)}, u32[]{:S(2)}, u32[]{:S(2)}) collective-permute-start(bf16[7,1,128,256]{3,2,1,0:T(8,128)(2,1)} %slice.70), channel_id=1, source_target_pairs={{32,0},{64,32},{96,64},{0,96},{33,1},{65,33},{97,65},{1,97},{34,2}... | collective-permute-start | bytes 1376264 | tf_op jit(solution)/shard_map/ppermute | solution.py:37
  106.7 17.5 %collective-permute-start.11 = (bf16[7,1,128,256]{3,2,1,0:T(8,128)(2,1)}, bf16[7,1,128,256]{3,2,1,0:T(8,128)(2,1)}, u32[]{:S(2)}, u32[]{:S(2)}) collective-permute-start(bf16[7,1,128,256]{3,2,1,0:T(8,128)(2,1)} %slice.71), channel_id=1, source_target_pairs={{96,0},{0,32},{32,64},{64,96},{97,1},{1,33},{33,65},{65,97},{98,2}... | collective-permute-start | bytes 1376264 | tf_op jit(solution)/shard_map/ppermute | solution.py:37
  117.0 110.3 %collective-permute-start.6 = (bf16[4,9,2,128,256]{4,3,2,1,0:T(8,128)(2,1)}, bf16[4,9,2,128,256]{4,3,2,1,0:T(8,128)(2,1)}, u32[]{:S(2)}, u32[]{:S(2)}) collective-permute-start(bf16[4,9,2,128,256]{4,3,2,1,0:T(8,128)(2,1)} %get-tuple-element.255), channel_id=1, source_target_pairs={{96,0},{0,32},{32,64},{64,96},{97,1},{1,33},{33,65},{65,97},{98,2}... | collective-permute-start | bytes 14155784 | tf_op jit(solution)/shard_map/ppermute | solution.py:37
  118.8 101.5 %collective-permute-start.4 = (bf16[4,9,2,128,256]{4,3,2,1,0:T(8,128)(2,1)}, bf16[4,9,2,128,256]{4,3,2,1,0:T(8,128)(2,1)}, u32[]{:S(2)}, u32[]{:S(2)}) collective-permute-start(bf16[4,9,2,128,256]{4,3,2,1,0:T(8,128)(2,1)} %get-tuple-element.255), channel_id=1, source_target_pairs={{32,0},{64,32},{96,64},{0,96},{33,1},{65,33},{97,65},{1,97},{34,2}... | collective-permute-start | bytes 14155784 | tf_op jit(solution)/shard_map/ppermute | solution.py:37
  128.6 83.7 %copy-start.4 = (bf16[4,7,2,128,256]{4,3,2,1,0:T(8,128)(2,1)S(1)}, bf16[4,7,2,128,256]{4,3,2,1,0:T(8,128)(2,1)}, u32[]{:S(2)}) copy-start(bf16[4,7,2,128,256]{4,3,2,1,0:T(8,128)(2,1)} %get-tuple-element.256) | copy-start | bytes 11010052
  128.6 78.9 %collective-permute-start.12 = (bf16[4,7,2,128,256]{4,3,2,1,0:T(8,128)(2,1)}, bf16[4,7,2,128,256]{4,3,2,1,0:T(8,128)(2,1)S(1)}, u32[]{:S(2)}, u32[]{:S(2)}) collective-permute-start(bf16[4,7,2,128,256]{4,3,2,1,0:T(8,128)(2,1)} %get-tuple-element.256), channel_id=1, source_target_pairs={{4,0},{8,4},{12,8},{0,12},{5,1},{9,5},{13,9},{1,13},{6,2},{10,6},{... | collective-permute-start | bytes 11010056 | tf_op jit(solution)/shard_map/ppermute | solution.py:37
  128.6 81.8 %collective-permute-start.14 = (bf16[4,7,2,128,256]{4,3,2,1,0:T(8,128)(2,1)}, bf16[4,7,2,128,256]{4,3,2,1,0:T(8,128)(2,1)S(1)}, u32[]{:S(2)}, u32[]{:S(2)}) collective-permute-start(bf16[4,7,2,128,256]{4,3,2,1,0:T(8,128)(2,1)} %get-tuple-element.256), channel_id=1, source_target_pairs={{12,0},{0,4},{4,8},{8,12},{13,1},{1,5},{5,9},{9,13},{14,2},{2,6},{... | collective-permute-start | bytes 11010056 | tf_op jit(solution)/shard_map/ppermute | solution.py:37
  208.9 38.8 %collective-permute-start.13 = (bf16[2,7,2,128,256]{4,3,2,1,0:T(8,128)(2,1)}, bf16[2,7,2,128,256]{4,3,2,1,0:T(8,128)(2,1)S(1)}, u32[]{:S(2)}, u32[]{:S(2)}) collective-permute-start(bf16[2,7,2,128,256]{4,3,2,1,0:T(8,128)(2,1)} %slice.72), channel_id=1, source_target_pairs={{4,0},{8,4},{12,8},{0,12},{5,1},{9,5},{13,9},{1,13},{6,2},{10,6},{... | collective-permute-start | bytes 5505032 | tf_op jit(solution)/shard_map/ppermute | solution.py:37
  211.9 40.0 %collective-permute-start.15 = (bf16[2,7,2,128,256]{4,3,2,1,0:T(8,128)(2,1)}, bf16[2,7,2,128,256]{4,3,2,1,0:T(8,128)(2,1)S(1)}, u32[]{:S(2)}, u32[]{:S(2)}) collective-permute-start(bf16[2,7,2,128,256]{4,3,2,1,0:T(8,128)(2,1)} %slice.73), channel_id=1, source_target_pairs={{12,0},{0,4},{4,8},{8,12},{13,1},{1,5},{5,9},{9,13},{14,2},{2,6},{... | collective-permute-start | bytes 5505032 | tf_op jit(solution)/shard_map/ppermute | solution.py:37
  223.6 51.5 %collective-permute-start.5 = (bf16[2,9,2,128,256]{4,3,2,1,0:T(8,128)(2,1)}, bf16[2,9,2,128,256]{4,3,2,1,0:T(8,128)(2,1)}, u32[]{:S(2)}, u32[]{:S(2)}) collective-permute-start(bf16[2,9,2,128,256]{4,3,2,1,0:T(8,128)(2,1)} %slice.67), channel_id=1, source_target_pairs={{32,0},{64,32},{96,64},{0,96},{33,1},{65,33},{97,65},{1,97},{34,2}... | collective-permute-start | bytes 7077896 | tf_op jit(solution)/shard_map/ppermute | solution.py:37
  230.7 51.2 %collective-permute-start.7 = (bf16[2,9,2,128,256]{4,3,2,1,0:T(8,128)(2,1)}, bf16[2,9,2,128,256]{4,3,2,1,0:T(8,128)(2,1)}, u32[]{:S(2)}, u32[]{:S(2)}) collective-permute-start(bf16[2,9,2,128,256]{4,3,2,1,0:T(8,128)(2,1)} %slice.68), channel_id=1, source_target_pairs={{96,0},{0,32},{32,64},{64,96},{97,1},{1,33},{33,65},{65,97},{98,2}... | collective-permute-start | bytes 7077896 | tf_op jit(solution)/shard_map/ppermute | solution.py:37
  284.7 2.4 slice-start
  285.4 2.6 slice-start.1
  285.4 3.3 %copy-start = (f32[9,2,64,512]{3,2,1,0:T(8,128)S(1)}, f32[9,2,64,512]{3,2,1,0:T(8,128)}, u32[]{:S(2)}) copy-start(f32[9,2,64,512]{3,2,1,0:T(8,128)} %convolution_bitcast_fusion) | copy-start | bytes 7077892
  285.4 3.9 %copy-start.1 = (f32[9,2,64,512]{3,2,1,0:T(8,128)S(1)}, f32[9,2,64,512]{3,2,1,0:T(8,128)}, u32[]{:S(2)}) copy-start(f32[9,2,64,512]{3,2,1,0:T(8,128)} %convolution_bitcast_fusion.2) | copy-start | bytes 7077892
